TPU v7x, 32 devices: a whole 2x2x4 slice. The times are simulated.
32 devices in a mesh: dp: 4 (over z), seq: 8 (over y, x, core).
Axes of the slice: x: 2, y: 2, z: 4, core: 2. Of those that a mesh axis runs over, the one named last changes fastest.
Arguments:
- features: bfloat16 [4, 1024, 6144], P('dp', 'seq'), may hold values from -6 to 6
- short_filter: float32 [3, 6144], replicated, may hold values from -3 to 3
- response: bfloat16 [1024, 2048], P('seq'), may hold values from -0.1875 to 0.1875
- skip_gain: float32 [2048], replicated, may hold values from -3 to 3
- cotangent: bfloat16 [4, 1024, 2048], P('dp', 'seq'), may hold values from -6 to 6
Outputs:
- gated: bfloat16 [4, 1024, 2048], P('dp', 'seq')
- grad_feats: bfloat16 [4, 1024, 6144], P('dp', 'seq')
- grad_short: float32 [3, 6144], replicated
- grad_skip: float32 [2048], replicated
- grad_response: float32 [1024, 2048], P('seq', 'dp')
All inputs are finite; a program needn't handle non-finite values.
Results may differ from a plain program's by a relative error of at most 0.0075.
Values may be sent and summed in bfloat16 or wider, within the bound.
No kernel may reach another device: no remote copies, remote signals or barrier semaphores. Data moves between devices by JAX's collectives and lax.ppermute only.
A program may use at most 128 MiB of HBM per device.

v0:
```python
import math

import jax
import jax.numpy as jnp
from jax import lax
from jax.sharding import PartitionSpec as P


precise = lax.Precision.HIGHEST


def dft_table(count):
    series = jnp.arange(count, dtype=jnp.int32)
    angle = (series[:, None] * series[None, :] % count).astype(jnp.float32) * (
        2.0 * math.pi / count
    )
    return (jnp.cos(angle), jnp.sin(angle))


def across_blocks(signal, offsets, blocks, fft_length):
    double = jnp.arange(2 * blocks, dtype=jnp.int32)
    single = jnp.arange(blocks, dtype=jnp.int32)
    angle = (double[:, None] * single[None, :] % (2 * blocks)).astype(jnp.float32) * (
        math.pi / blocks
    )
    table = jnp.stack([jnp.cos(angle), -jnp.sin(angle)])
    first = jnp.einsum("oap,bpjk->obajk", table, signal, precision=precise)
    twist = (double[:, None] * offsets[None, :] % fft_length).astype(jnp.float32) * (
        -2.0 * math.pi / fft_length
    )
    cosine = jnp.cos(twist)[None, :, :, None]
    sine = jnp.sin(twist)[None, :, :, None]
    return (first[0] * cosine - first[1] * sine, first[0] * sine + first[1] * cosine)


def within_blocks(part_real, part_imag):
    table_cos, table_sin = dft_table(part_real.shape[2])
    table = jnp.stack([jnp.stack([table_cos, table_sin]), jnp.stack([-table_sin, table_cos])])
    spectra = jnp.einsum(
        "oibj,ixajk->oxabk", table, jnp.stack([part_real, part_imag]), precision=precise
    )
    return (spectra[0], spectra[1])


def back_within(spec_real, spec_imag, firsts, fft_length):
    count = spec_real.shape[2]
    table_cos, table_sin = dft_table(count)
    table = jnp.stack([jnp.stack([table_cos, -table_sin]), jnp.stack([table_sin, table_cos])])
    backs = jnp.einsum(
        "oibj,ixabk->oxajk", table, jnp.stack([spec_real, spec_imag]), precision=precise
    )
    series = jnp.arange(count, dtype=jnp.int32)
    twist = (firsts[:, None] * series[None, :] % fft_length).astype(jnp.float32) * (
        2.0 * math.pi / fft_length
    )
    cosine = jnp.cos(twist)[None, :, :, None]
    sine = jnp.sin(twist)[None, :, :, None]
    return (backs[0] * cosine - backs[1] * sine, backs[0] * sine + backs[1] * cosine)


def back_across(part_real, part_imag, blocks, fft_length):
    double = jnp.arange(2 * blocks, dtype=jnp.int32)
    single = jnp.arange(blocks, dtype=jnp.int32)
    angle = (single[:, None] * double[None, :] % (2 * blocks)).astype(jnp.float32) * (
        math.pi / blocks
    )
    table = jnp.stack([jnp.cos(angle), -jnp.sin(angle)])
    result = jnp.einsum(
        "ipa,ibajk->bpjk", table, jnp.stack([part_real, part_imag]), precision=precise
    )
    return result * (1.0 / fft_length)


def times_spectrum(left, right):
    return (left[0] * right[0] - left[1] * right[1], left[0] * right[1] + left[1] * right[0])


def times_conjugate(left, right):
    return (left[0] * right[0] + left[1] * right[1], left[1] * right[0] - left[0] * right[1])


def blocked_core(extended, cotangent, taps, skip_gain, response, to_spectrum, to_signal, after_rows):
    count = cotangent.shape[1]
    batch = cotangent.shape[0]
    mixed = taps[0] * extended[:, 2:] + taps[1] * extended[:, 1:-1] + taps[2] * extended[:, :-2]
    query_feat = mixed[:, :, 0]
    key_feat = mixed[:, :, 1]
    value_feat = mixed[:, :, 2]
    product = (key_feat * value_feat).astype(jnp.bfloat16)
    stacked = to_spectrum(jnp.concatenate([product, response[None]], axis=0))
    prod_spec = (stacked[0][:batch], stacked[1][:batch])
    resp_spec = (stacked[0][batch:], stacked[1][batch:])
    conv_out = to_signal(times_spectrum(prod_spec, resp_spec))
    carried = conv_out + skip_gain * product
    gated = (query_feat * carried).astype(jnp.bfloat16)
    grad_carried = (cotangent * query_feat).astype(jnp.bfloat16)
    grad_query = cotangent * carried
    grad_spec = to_spectrum(grad_carried)
    back_conv = times_conjugate(grad_spec, resp_spec)
    resp_grad = times_conjugate(grad_spec, prod_spec)
    joined_real = jnp.concatenate(
        [back_conv[0], jnp.sum(resp_grad[0], axis=0, keepdims=True)], axis=0
    )
    joined_imag = jnp.concatenate(
        [back_conv[1], jnp.sum(resp_grad[1], axis=0, keepdims=True)], axis=0
    )
    both = to_signal((joined_real, joined_imag))
    grad_product = both[:batch] + skip_gain * grad_carried
    grad_mixed = jnp.stack([grad_query, grad_product * value_feat, grad_product * key_feat], axis=2)
    tail = jnp.concatenate([grad_mixed, after_rows(grad_mixed[:, :2])], axis=1)
    grad_feats = (
        taps[0] * tail[:, :count] + taps[1] * tail[:, 1 : count + 1] + taps[2] * tail[:, 2:]
    ).astype(jnp.bfloat16)
    grad_taps = jnp.stack(
        [
            jnp.sum(grad_mixed * extended[:, 2 - tap_index : 2 - tap_index + count], axis=(0, 1))
            for tap_index in range(3)
        ]
    )
    grad_skip = jnp.sum(grad_carried.astype(jnp.float32) * product.astype(jnp.float32), axis=(0, 1))
    return (gated, grad_feats, grad_taps, grad_skip, both[batch])


def dft_tables(length):
    fft_length = 2 * length
    bins = length + 1
    freq = lax.broadcasted_iota(jnp.int32, (bins, length), 0)
    time = lax.broadcasted_iota(jnp.int32, (bins, length), 1)
    angle = lax.optimization_barrier((freq * time) % fft_length).astype(jnp.float32) * (
        2.0 * math.pi / fft_length
    )
    table = jnp.concatenate([jnp.cos(angle), -jnp.sin(angle)], axis=0)
    high = table.astype(jnp.bfloat16)
    low = (table - high.astype(jnp.float32)).astype(jnp.bfloat16)
    return high, low


def bf16_dot(left, right, dims):
    return lax.dot_general(left, right, (dims, ((), ())), preferred_element_type=jnp.float32)


def to_spectrum(tables, signal):
    high, low = tables
    forward = ((1,), (0,))
    return bf16_dot(high, signal, forward) + bf16_dot(low, signal, forward)


def to_signal(tables, spectrum):
    high, low = tables
    bins = high.shape[0] // 2
    fft_length = 2 * (bins - 1)
    row = lax.broadcasted_iota(jnp.int32, (2 * bins, 1), 0)
    edge = (row == 0) | (row == bins - 1) | (row == bins) | (row == 2 * bins - 1)
    weight = jnp.where(edge, 1.0 / fft_length, 2.0 / fft_length)
    scaled = spectrum * weight
    spec_high = scaled.astype(jnp.bfloat16)
    spec_low = (scaled - spec_high.astype(jnp.float32)).astype(jnp.bfloat16)
    backward = ((0,), (0,))
    return (
        bf16_dot(high, spec_high, backward)
        + bf16_dot(high, spec_low, backward)
        + bf16_dot(low, spec_high, backward)
    )


def split(spectrum):
    bins = spectrum.shape[0] // 2
    return spectrum[:bins], spectrum[bins:]


def join(real, imag):
    return jnp.concatenate([real, imag], axis=0)


def block_core(feats, cot, resp, taps, skip_gain):
    length = feats.shape[0]
    narrow = feats.shape[2]
    tables = dft_tables(length)
    extended = jnp.concatenate([jnp.zeros((2, 3, narrow), feats.dtype), feats], axis=0)
    mixed = taps[0] * extended[2:] + taps[1] * extended[1:-1] + taps[2] * extended[:-2]
    query_feat = mixed[:, 0]
    key_feat = mixed[:, 1]
    value_feat = mixed[:, 2]
    product = (key_feat * value_feat).astype(jnp.bfloat16)
    first = to_spectrum(tables, jnp.concatenate([product, resp], axis=1))
    prod_re, prod_im = split(first[:, :narrow])
    resp_re, resp_im = split(first[:, narrow:])
    conv_out = to_signal(
        tables, join(prod_re * resp_re - prod_im * resp_im, prod_re * resp_im + prod_im * resp_re)
    )
    carried = conv_out + skip_gain * product
    gated = (query_feat * carried).astype(jnp.bfloat16)
    grad_carried = (cot * query_feat).astype(jnp.bfloat16)
    grad_query = cot * carried
    grad_re, grad_im = split(to_spectrum(tables, grad_carried))
    back_spec = join(grad_re * resp_re + grad_im * resp_im, grad_im * resp_re - grad_re * resp_im)
    filt_spec = join(grad_re * prod_re + grad_im * prod_im, grad_im * prod_re - grad_re * prod_im)
    both = to_signal(tables, jnp.concatenate([back_spec, filt_spec], axis=1))
    grad_product = both[:, :narrow] + skip_gain * grad_carried
    grad_mixed = jnp.stack([grad_query, grad_product * value_feat, grad_product * key_feat], axis=1)
    tail = jnp.concatenate([grad_mixed, jnp.zeros((2, 3, narrow), jnp.float32)], axis=0)
    grad_feats = (
        taps[0] * tail[:length] + taps[1] * tail[1 : length + 1] + taps[2] * tail[2:]
    ).astype(jnp.bfloat16)
    grad_taps = jnp.stack(
        [
            jnp.sum(grad_mixed * extended[2 - tap_index : 2 - tap_index + length], axis=0)
            for tap_index in range(3)
        ]
    )
    grad_skip = jnp.sum(grad_carried.astype(jnp.float32) * product.astype(jnp.float32), axis=0)
    return gated, grad_feats, grad_taps, grad_skip, both[:, narrow:]


def blocked_fallback(moved_in, taps, skip_gain, seq_parts, tok_rows, narrow):
    length = seq_parts * tok_rows
    fft_length = 2 * length
    local_feats = moved_in[None, :, :3]
    extended = jnp.concatenate(
        [jnp.zeros((1, 2, 3, narrow), local_feats.dtype), local_feats], axis=1
    )

    def local_spectrum(signal):
        blocks = signal.reshape(signal.shape[0], seq_parts, tok_rows, narrow).astype(jnp.float32)
        part_real, part_imag = across_blocks(
            blocks, jnp.arange(tok_rows, dtype=jnp.int32), seq_parts, fft_length
        )
        return within_blocks(part_real, part_imag)

    def local_signal(spectrum):
        part_real, part_imag = back_within(
            spectrum[0], spectrum[1], jnp.arange(2 * seq_parts, dtype=jnp.int32), fft_length
        )
        values = back_across(part_real, part_imag, seq_parts, fft_length)
        return values.reshape(values.shape[0], length, narrow)

    def no_rows(rows_part):
        return jnp.zeros_like(rows_part)

    return blocked_core(
        extended,
        moved_in[None, :, 3],
        taps,
        skip_gain,
        moved_in[:, 4],
        local_spectrum,
        local_signal,
        no_rows,
    )


def local(features, short_filter, response, skip_gain, cotangent):
    seq_parts = lax.axis_size("seq")
    dp_parts = lax.axis_size("dp")
    seq_index = lax.axis_index("seq")
    tok_rows = features.shape[1]
    chan_width = features.shape[2] // 3
    length = seq_parts * tok_rows
    narrow = chan_width // seq_parts
    offset = seq_index * narrow
    taps = short_filter.reshape(3, 3, chan_width)
    joined_in = jnp.concatenate(
        [
            features.reshape(tok_rows, 3 * chan_width),
            cotangent.reshape(tok_rows, chan_width),
            response,
        ],
        axis=1,
    )
    arranged = joined_in.reshape(tok_rows, 5, seq_parts, narrow).transpose(2, 0, 1, 3)
    moved_in = lax.all_to_all(arranged, "seq", 0, 0, tiled=True).reshape(length, 5, narrow)
    local_taps = lax.dynamic_slice_in_dim(taps, offset, narrow, 2)
    local_skip = lax.dynamic_slice_in_dim(skip_gain, offset, narrow, 0)
    if length <= 2048:
        gated, grad_feats, grad_taps, grad_skip, filter_part = block_core(
            moved_in[:, :3], moved_in[:, 3], moved_in[:, 4], local_taps, local_skip
        )
    else:
        gated, grad_feats, grad_taps, grad_skip, filter_part = blocked_fallback(
            moved_in, local_taps, local_skip, seq_parts, tok_rows, narrow
        )
        gated = gated.reshape(length, narrow)
        grad_feats = grad_feats.reshape(length, 3, narrow)
    joined_out = jnp.concatenate(
        [gated.reshape(seq_parts, tok_rows, 1, narrow), grad_feats.reshape(seq_parts, tok_rows, 3, narrow)],
        axis=2,
    )
    moved_out = lax.all_to_all(joined_out, "seq", 0, 0, tiled=True).transpose(1, 2, 0, 3)
    gated = moved_out[:, 0]
    grad_feats = moved_out[:, 1:]
    extra = 16
    small = jnp.concatenate(
        [grad_taps.reshape(9, narrow), grad_skip[None], jnp.zeros((extra - 10, narrow), jnp.float32)],
        axis=0,
    )
    chunks = jnp.concatenate(
        [
            filter_part.reshape(seq_parts, tok_rows, narrow),
            jnp.broadcast_to(small[None], (seq_parts, extra, narrow)),
        ],
        axis=1,
    )
    moved = (
        lax.all_to_all(chunks, "seq", 0, 0, tiled=True)
        .transpose(1, 0, 2)
        .reshape(tok_rows + extra, chan_width)
    )
    block = chan_width // dp_parts
    small_all = moved[tok_rows : tok_rows + 10]
    small_rows = small_all.reshape(10, dp_parts, block).transpose(1, 0, 2).reshape(dp_parts * 10, block)
    joined = jnp.concatenate([moved[:tok_rows], jnp.tile(small_rows, (1, dp_parts))], axis=0)
    reduced = lax.psum_scatter(joined, "dp", scatter_dimension=1, tiled=True)
    filter_total = reduced[:tok_rows]
    small_total = (
        reduced[tok_rows:].reshape(dp_parts, 10, block).transpose(1, 0, 2).reshape(10, chan_width)
    )
    gated = gated.reshape(1, tok_rows, chan_width)
    grad_feats = grad_feats.reshape(1, tok_rows, 3 * chan_width)
    return (
        gated,
        grad_feats,
        small_total[:9].reshape(3, 3 * chan_width),
        small_total[9],
        filter_total,
    )


def solution(mesh):
    placed = (P("dp", "seq", None), P(), P("seq", None), P(), P("dp", "seq", None))
    return jax.shard_map(
        local,
        mesh=mesh,
        in_specs=placed,
        out_specs=(P("dp", "seq", None), P("dp", "seq", None), P(), P(), P("seq", "dp")),
        check_vma=False,
    )
```

profile of v0, /device:TPU:0, one launch (start us, length us, event | category | flops | bytes accessed | tf_op | source)
XLA Modules:
  0.0 171.7 jit_solution(16831732897377665886)
XLA Ops:
  7.2 2.7 %copy.32 = bf16[1,128,6144]{1,2,0:T(8,128)(2,1)} copy(bf16[1,128,6144]{2,1,0:T(8,128)(2,1)} %param.5) | data formatting | bytes 3145728 | tf_op args[0]
  9.9 0.3 copy.33
  10.1 1.0 copy.34
  11.1 5.6 %pad_maximum_fusion.4 = bf16[128,10240]{0,1:T(8,128)(2,1)S(1)} fusion(bf16[128,2048]{0,1:T(8,128)(2,1)} %copy.34, bf16[128,2048]{0,1:T(8,128)(2,1)S(1)} %bitcast.102, bf16[128,6144]{0,1:T(8,128)(2,1)} %bitcast.94), kind=kLoop, calls=%fused_computation.33 | loop fusion | flops 7864320 | bytes 5242880 | tf_op jit(solution)/shard_map/concatenate | solution.py:262
  16.8 2.6 %copy.35 = bf16[8,128,5,256]{3,1,2,0:T(8,128)(2,1)} copy(bf16[8,128,5,256]{1,3,0,2:T(8,128)(2,1)S(1)} %bitcast.88) | data formatting | bytes 5242880 | tf_op jit(solution)/shard_map/transpose | solution.py:270
  19.4 5.2 %all-to-all-start = ((bf16[8,128,5,256]{3,1,2,0:T(8,128)(2,1)}), bf16[8,128,5,256]{3,1,2,0:T(8,128)(2,1)S(1)}, u32[]{:S(2)}, u32[]{:S(2)}) async-start(bf16[8,128,5,256]{3,1,2,0:T(8,128)(2,1)} %copy.35), calls=%async_computation | async-start | bytes 5242880 | tf_op jit(solution)/shard_map/all_to_all | solution.py:271
  24.6 3.7 %add_select_fusion = s32[1025,1024]{1,0:T(8,128)} fusion(), kind=kLoop, calls=%fused_computation.3 | loop fusion | flops 12595200 | bytes 4198400 | tf_op jit(solution)/shard_map/jit(remainder)/select_n | solution.py:129
  28.4 0.8 dynamic_slice.7
  29.3 16.2 %fusion.7 = (f32[1025,1024]{1,0:T(8,128)S(1)}, f32[1025,1024]{1,0:T(8,128)S(1)}) fusion(s32[1025,1024]{1,0:T(8,128)} %add_select_fusion), kind=kLoop, calls=%fused_computation.19 | loop fusion | flops 3148800 | bytes 12595200 | tf_op jit(solution)/shard_map/cos | solution.py:132
  45.5 4.1 %subtract_convert_fusion = (bf16[2050,1024]{1,0:T(8,128)(2,1)}, bf16[2050,1024]{1,0:T(8,128)(2,1)}) fusion(f32[1025,1024]{1,0:T(8,128)S(1)} %get-tuple-element.25, f32[1025,1024]{1,0:T(8,128)S(1)} %get-tuple-element.24), kind=kLoop, calls=%fused_computation.1 | loop fusion | flops 16793600 | bytes 16793600 | tf_op jit(solution)/shard_map/convert_element_type | solution.py:134
  49.6 7.2 %all-to-all-done = bf16[8,128,5,256]{3,1,2,0:T(8,128)(2,1)S(1)} async-done(((bf16[8,128,5,256]{3,1,2,0:T(8,128)(2,1)}), bf16[8,128,5,256]{3,1,2,0:T(8,128)(2,1)S(1)}, u32[]{:S(2)}, u32[]{:S(2)}) %all-to-all-start) | async-done | bytes 2621472 | tf_op jit(solution)/shard_map/all_to_all | solution.py:271
  56.8 0.2 copy.36
  57.2 1.0 fusion.9
  58.2 0.4 fusion.20
  58.6 0.7 slice-done.2
  59.3 2.4 %fusion.23 = f32[2050,512]{1,0:T(8,128)S(1)} fusion(bf16[2050,1024]{1,0:T(8,128)(2,1)S(1)} %bitcast.97, bf16[1024,256]{1,0:T(8,128)(2,1)S(1)} %slice_bitcast_fusion.4, bf16[1024,256]{1,0:T(8,128)(2,1)S(1)} %get-tuple-element.14), kind=kOutput, calls=%fused_computation.73 | convolution fusion | flops 2151677952 | bytes 9445376 | tf_op jit(solution)/shard_map/dot_general | solution.py:139
  61.8 2.6 %convolution_add_fusion = f32[2050,512]{1,0:T(8,128)S(1)} fusion(f32[2050,512]{1,0:T(8,128)S(1)} %fusion.23, bf16[2050,1024]{1,0:T(8,128)(2,1)S(1)} %bitcast.82, bf16[1024,256]{1,0:T(8,128)(2,1)S(1)} %slice_bitcast_fusion.4, bf16[1024,256]{1,0:T(8,128)(2,1)S(1)} %get-tuple-element.14), kind=kOutput, calls=%fused_computation.6 | convolution fusion | flops 2152727552 | bytes 13643776 | tf_op jit(solution)/shard_map/dot_general | solution.py:139
  64.4 0.3 multiply_subtract_fusion.2
  64.8 1.4 fusion.43
  66.2 1.5 convolution_add_fusion.1
  67.7 0.7 multiply_add_fusion.1
  68.4 2.8 %fusion.39 = f32[1024,512]{1,0:T(8,128)S(1)} fusion(bf16[2050,1024]{1,0:T(8,128)(2,1)S(1)} %bitcast.97, f32[1025,256]{1,0:T(8,128)S(1)} %get-tuple-element.20, f32[1025,256]{1,0:T(8,128)S(1)} %get-tuple-element.19, f32[1025,256]{1,0:T(8,128)S(1)} %get-tuple-element.21, f32[1025,256]{1,0:T(8,128)S(1)} %get-tuple-element.18, f32[2050]{0:T(1024)S(1)} %fusion.27), kind=kOutput, calls=%fused_computation.95 | convolution fusion | flops 2154828800 | bytes 10502152 | tf_op jit(solution)/shard_map/dot_general | solution.py:139
  71.1 3.0 %fusion.36 = f32[1024,512]{1,0:T(8,128)S(1)} fusion(bf16[2050,1024]{1,0:T(8,128)(2,1)S(1)} %bitcast.82, f32[1025,256]{1,0:T(8,128)S(1)} %get-tuple-element.20, f32[1025,256]{1,0:T(8,128)S(1)} %get-tuple-element.19, f32[1025,256]{1,0:T(8,128)S(1)} %get-tuple-element.21, f32[1025,256]{1,0:T(8,128)S(1)} %get-tuple-element.18, f32[2050]{0:T(1024)S(1)} %fusion.27), kind=kOutput, calls=%fused_computation.94 | convolution fusion | flops 2154828800 | bytes 10502152 | tf_op jit(solution)/shard_map/dot_general | solution.py:139
  74.2 2.0 %fusion.34 = f32[1024,256]{1,0:T(8,128)S(1)} fusion(bf16[2050,1024]{1,0:T(8,128)(2,1)S(1)} %bitcast.97, f32[1025,256]{1,0:T(8,128)S(1)} %get-tuple-element.27, f32[1025,256]{1,0:T(8,128)S(1)} %get-tuple-element.26, f32[2050]{0:T(1024)S(1)} %fusion.27), kind=kOutput, calls=%fused_computation.93 | convolution fusion | flops 1076364800 | bytes 7354376 | tf_op jit(solution)/shard_map/dot_general | solution.py:139
  76.2 2.0 %convolution_add_fusion.3 = f32[1024,256]{1,0:T(8,128)S(1)} fusion(f32[1024,256]{1,0:T(8,128)S(1)} %fusion.34, bf16[2050,1024]{1,0:T(8,128)(2,1)S(1)} %bitcast.97, f32[1025,256]{1,0:T(8,128)S(1)} %get-tuple-element.27, f32[1025,256]{1,0:T(8,128)S(1)} %get-tuple-element.26, f32[2050]{0:T(1024)S(1)} %fusion.27), kind=kOutput, calls=%fused_computation.51 | convolution fusion | flops 1078201344 | bytes 8402952 | tf_op jit(solution)/shard_map/dot_general | solution.py:139
  78.2 2.0 %fusion.17 = f32[1024,256]{1,0:T(8,128)S(1)} fusion(f32[1024,256]{1,0:T(8,128)S(1)} %convolution_add_fusion.3, bf16[2050,1024]{1,0:T(8,128)(2,1)S(1)} %bitcast.82, bf16[1024,256]{1,0:T(8,128)(2,1)S(1)} %get-tuple-element.14, f32[256]{0:T(256)S(1)} %dynamic_slice.7, f32[1025,256]{1,0:T(8,128)S(1)} %get-tuple-element.27, ...), kind=kOutput, calls=%fused_computation.52 | convolution fusion | flops 1077413376 | bytes 8928264 | tf_op jit(solution)/shard_map/dot_general | solution.py:139
  80.4 2.8 %add_add_fusion = f32[1024,512]{1,0:T(8,128)S(1)} fusion(f32[1024,512]{1,0:T(8,128)S(1)} %fusion.36, f32[1024,512]{1,0:T(8,128)S(1)} %fusion.39, bf16[2050,1024]{1,0:T(8,128)(2,1)S(1)} %bitcast.97, f32[1025,256]{1,0:T(8,128)S(1)} %get-tuple-element.20, f32[1025,256]{1,0:T(8,128)S(1)} %get-tuple-element.19, f32[1025,256]{1,0:T(8,128)S(1)} %get-tuple-element.21, ...), kind=kOutput, calls=%fused_computation.41 | convolution fusion | flops 2159026176 | bytes 14696456 | tf_op jit(solution)/shard_map/dot_general | solution.py:139
  83.2 1.5 multiply_bitcast_fusion.1
  84.8 1.3 fusion.11
  86.2 1.3 pad_maximum_fusion.7
  87.5 19.9 %all_to_all.15 = f32[8,144,256]{2,1,0:T(8,128)} all-to-all(f32[8,144,256]{2,1,0:T(8,128)S(1)} %pad_maximum_fusion.7), channel_id=1, replica_groups=mesh['dp'=4,'seq'=8] {'seq'}, dimensions={0} | all-to-all | bytes 2359296 | tf_op jit(solution)/shard_map/all_to_all | solution.py:304
  107.3 2.8 %copy.40 = f32[8,144,256]{1,2,0:T(8,128)} copy(f32[8,144,256]{2,1,0:T(8,128)} %all_to_all.15) | data formatting | bytes 2359296 | tf_op jit(solution)/shard_map/all_to_all | solution.py:304
  110.1 2.4 %slice.151 = f32[10,8,256]{0,2,1:T(8,128)} slice(f32[144,8,256]{0,2,1:T(8,128)} %bitcast.91), slice={[128:138], [0:8], [0:256]} | slice | bytes 163840 | tf_op jit(solution)/shard_map/slice | solution.py:309
  112.5 1.0 slice.150
  113.6 1.5 copy.49
  115.4 2.7 %pad_maximum_fusion.6 = f32[168,2048]{0,1:T(8,128)} fusion(f32[40,2048]{0,1:T(8,128)S(1)} %bitcast.99, f32[128,2048]{0,1:T(8,128)} %bitcast.100), kind=kLoop, calls=%fused_computation.40 | loop fusion | flops 344064 | bytes 2752512 | tf_op jit(solution)/shard_map/concatenate | solution.py:311
  118.1 1.0 add_convert_fusion
  119.2 0.2 pad_maximum_fusion.5
  119.4 29.8 %all_to_all.16 = bf16[8,128,4,256]{3,1,2,0:T(8,128)(2,1)} all-to-all(bf16[8,128,4,256]{3,1,2,0:T(8,128)(2,1)S(1)} %pad_maximum_fusion.5), channel_id=1, replica_groups=mesh['dp'=4,'seq'=8] {'seq'}, dimensions={0} | all-to-all | bytes 4194304 | tf_op jit(solution)/shard_map/all_to_all | solution.py:288
  149.1 3.0 %copy.39 = bf16[8,128,4,256]{1,3,0,2:T(8,128)(2,1)S(1)} copy(bf16[8,128,4,256]{3,1,2,0:T(8,128)(2,1)} %all_to_all.16) | data formatting | bytes 4194304 | tf_op jit(solution)/shard_map/all_to_all | solution.py:288
  152.2 1.3 slice.148
  153.5 2.6 %copy.47 = bf16[1,128,6144]{2,1,0:T(8,128)(2,1)} copy(bf16[1,128,6144]{1,2,0:T(8,128)(2,1)} %bitcast.93) | data formatting | bytes 3145728
  156.1 1.0 copy.46
  157.1 4.4 %reduce-scatter.2.cloned.1.call-done = f32[168,512]{0,1:T(8,128)} async-done(((f32[168,2048]{0,1:T(8,128)}), f32[168,512]{0,1:T(8,128)}) %reduce-scatter.2.cloned.1.call-update) | async-done | bytes 344080 | tf_op jit(solution)/shard_map/reduce_scatter | solution.py:312
  161.5 1.0 slice.152
  162.6 0.6 slice.154
  163.3 0.7 reshape.103
  164.0 0.8 copy.48
  (43 shorter events, 1.1 us)
Async XLA Ops:
  7.2 2.7 %copy-start.2 = (bf16[1,128,2048]{2,1,0:T(8,128)(2,1)S(1)}, bf16[1,128,2048]{2,1,0:T(8,128)(2,1)}, u32[]{:S(2)}) copy-start(bf16[1,128,2048]{2,1,0:T(8,128)(2,1)} %param.9) | copy-start | bytes 1572868
  7.2 3.0 %copy-start.3 = (bf16[128,2048]{1,0:T(8,128)(2,1)S(1)}, bf16[128,2048]{1,0:T(8,128)(2,1)}, u32[]{:S(2)}) copy-start(bf16[128,2048]{1,0:T(8,128)(2,1)} %param.7) | copy-start | bytes 1572868
  19.4 37.4 %all-to-all-start = ((bf16[8,128,5,256]{3,1,2,0:T(8,128)(2,1)}), bf16[8,128,5,256]{3,1,2,0:T(8,128)(2,1)S(1)}, u32[]{:S(2)}, u32[]{:S(2)}) async-start(bf16[8,128,5,256]{3,1,2,0:T(8,128)(2,1)} %copy.35), calls=%async_computation | async-start | bytes 5242880 | tf_op jit(solution)/shard_map/all_to_all | solution.py:271
  24.6 3.8 %copy-start.4 = (f32[3,6144]{1,0:T(4,128)S(1)}, f32[3,6144]{1,0:T(4,128)}, u32[]{:S(2)}) copy-start(f32[3,6144]{1,0:T(4,128)} %param.6) | copy-start | bytes 221188
  24.6 136.9 %reduce-scatter.2.cloned.1.call-start = ((), (), s32[]{:S(2)}) async-start(), calls=%async_computation.4 | async-start | bytes 2621440 | tf_op jit(solution)/shard_map/reduce_scatter | solution.py:312
  57.1 2.2 %slice-start.2 = ((s8[4210688]{0:T(1024)(128)(4,1)}), s8[4194304]{0:T(1024)(128)(4,1)S(1)}, s32[]{:S(2)}) async-start(s8[4210688]{0:T(1024)(128)(4,1)} %bitcast.96), calls=%async_computation.7 | async-start | bytes 8388608
  57.2 2.1 %slice-start.3 = ((s8[4210688]{0:T(1024)(128)(4,1)}), s8[16384]{0:T(1024)(128)(4,1)S(1)}, s32[]{:S(2)}) async-start(s8[4210688]{0:T(1024)(128)(4,1)} %bitcast.96), calls=%async_computation.8 | async-start | bytes 32768
  58.2 3.6 %slice-start = ((s8[4210688]{0:T(1024)(128)(4,1)}), s8[4194304]{0:T(1024)(128)(4,1)S(1)}, s32[]{:S(2)}) async-start(s8[4210688]{0:T(1024)(128)(4,1)} %bitcast.81), calls=%async_computation.5 | async-start | bytes 8388608
  59.3 2.5 %slice-start.1 = ((s8[4210688]{0:T(1024)(128)(4,1)}), s8[16384]{0:T(1024)(128)(4,1)S(1)}, s32[]{:S(2)}) async-start(s8[4210688]{0:T(1024)(128)(4,1)} %bitcast.81), calls=%async_computation.6 | async-start | bytes 32768
  110.1 2.4 %copy-start = (f32[8,144,256]{1,2,0:T(8,128)S(1)}, f32[8,144,256]{1,2,0:T(8,128)}, u32[]{:S(2)}) copy-start(f32[8,144,256]{1,2,0:T(8,128)} %copy.40) | copy-start | bytes 3538948
  118.1 1.0 copy-start.1
  161.5 2.5 %slice-start.4 = ((f32[168,512]{0,1:T(8,128)}), f32[128,512]{0,1:T(8,128)S(1)}, s32[]{:S(2)}) async-start(f32[168,512]{0,1:T(8,128)} %reduce-scatter.2.cloned.1.call-done), calls=%async_computation.9 | async-start | bytes 524288 | tf_op jit(solution)/shard_map/slice | solution.py:313
Sparse Core Ops, SparseCore 0:
  118.2 43.1 reduce-scatter.1
where the time goes:
time: 172 us
  blocking collectives  49.6 us (29%)
  other arithmetic  40.2 us (23%)
  local copies, waits for them, and re-layouts  27.9 us (16%)
  matrix products  22.7 us (13%)
  between operations  14.4 us (8%)
  waiting for transfers between devices  11.6 us (7%)
  starting transfers between devices  5.21 us (3%)
    all_to_all x1, blocking collectives, local(): lax.all_to_all(joined_out, 'seq', 0, 0, tiled=True).transpose(1, 2, 0, 3)  29.8 us
    dot_general x10, matrix products, bf16_dot(): lax.dot_general(left, right, (dims, ((), ())), preferred_element_type=jnp...  22.7 us
    all_to_all x1, blocking collectives, local(): lax.all_to_all(chunks, 'seq', 0, 0, tiled=True).transpose(1, 0, 2)  19.9 us
    cos x1, other arithmetic, dft_tables(): table = jnp.concatenate([jnp.cos(angle), -jnp.sin(angle)], axis=0)  16.2 us
    unnamed x24, local copies, waits for them, and re-layouts  9.18 us
    all_to_all x1, waiting for transfers between devices, local(): lax.all_to_all(arranged, 'seq', 0, 0, tiled=True).reshape(length, 5, narrow)  7.22 us
    concatenate x1, other arithmetic, local(): jnp.concatenate([features.reshape(tok_rows, 3 * chan_width), cotangent.re...  5.61 us
    all_to_all x1, starting transfers between devices, local(): lax.all_to_all(arranged, 'seq', 0, 0, tiled=True).reshape(length, 5, narrow)  5.17 us
  transfers between devices with their start and end apart: 2, of which 2 were waited for; matrix products, arithmetic and copies ran while one was open for 20% of the time, Pallas kernels for 0%

commit v1 on v0

--- a/solution.py
+++ b/solution.py
@@ -300,19 +300,24 @@
         ],
         axis=1,
     )
-    moved = (
-        lax.all_to_all(chunks, "seq", 0, 0, tiled=True)
-        .transpose(1, 0, 2)
-        .reshape(tok_rows + extra, chan_width)
-    )
-    block = chan_width // dp_parts
-    small_all = moved[tok_rows : tok_rows + 10]
-    small_rows = small_all.reshape(10, dp_parts, block).transpose(1, 0, 2).reshape(dp_parts * 10, block)
-    joined = jnp.concatenate([moved[:tok_rows], jnp.tile(small_rows, (1, dp_parts))], axis=0)
-    reduced = lax.psum_scatter(joined, "dp", scatter_dimension=1, tiled=True)
-    filter_total = reduced[:tok_rows]
+    moved = lax.all_to_all(chunks, "seq", 0, 0, tiled=True)
+    pair = seq_parts // dp_parts
+    small_all = moved[:, tok_rows : tok_rows + 10]
+    small_rows = (
+        small_all.reshape(dp_parts, pair, 10, narrow)
+        .transpose(1, 0, 2, 3)
+        .reshape(pair, dp_parts * 10, narrow)
+    )
+    joined = jnp.concatenate(
+        [moved[:, :tok_rows], jnp.tile(small_rows, (dp_parts, 1, 1))], axis=1
+    )
+    reduced = lax.psum_scatter(joined, "dp", scatter_dimension=0, tiled=True)
+    filter_total = reduced[:, :tok_rows].transpose(1, 0, 2).reshape(tok_rows, pair * narrow)
     small_total = (
-        reduced[tok_rows:].reshape(dp_parts, 10, block).transpose(1, 0, 2).reshape(10, chan_width)
+        reduced[:, tok_rows:]
+        .reshape(pair, dp_parts, 10, narrow)
+        .transpose(2, 1, 0, 3)
+        .reshape(10, chan_width)
     )
     gated = gated.reshape(1, tok_rows, chan_width)
     grad_feats = grad_feats.reshape(1, tok_rows, 3 * chan_width)

time: 172 us -> 159 us (0.924)
  local copies, waits for them, and re-layouts: 27.9 us -> 21 us
  waiting for transfers between devices: 11.6 us -> 7.23 us
    reduce_scatter x1, waiting for transfers between devices: 4.4 us -> 0.01 us  [local(): reduced = lax.psum_scatter(joined, 'dp', scatter_dimension=0, tiled=True)]
    slice x7 -> x5, local copies, waits for them, and re-layouts: 5.18 us -> 1.99 us  [the longest x1 0.97 us: local(): reduced[:, :tok_rows].transpose(1, 0, 2).reshape(tok_rows, pair * narrow)]
    all_to_all x1 -> x0, local copies, waits for them, and re-layouts: 2.75 us -> none  [local(): lax.all_to_all(chunks, 'seq', 0, 0, tiled=True).transpose(1, 0, 2)]
    unnamed x24 -> x25, local copies, waits for them, and re-layouts: 9.18 us -> 9.91 us
  transfers between devices with their start and end apart: 2 -> 2, of which waited for: 2 -> 1; matrix products, arithmetic and copies ran while one was open for 20% -> 22% of each run, Pallas kernels for 0% -> 0%
where the time goes in v1:
time: 159 us; the launch traced here: 158 us
  blocking collectives  48.9 us (31%)
  other arithmetic  38.7 us (24%)
  matrix products  22.7 us (14%)
  local copies, waits for them, and re-layouts  21 us (13%)
  between operations  14.4 us (9%)
  waiting for transfers between devices  7.23 us (5%)
  starting transfers between devices  5.21 us (3%)
    all_to_all x1, blocking collectives, local(): lax.all_to_all(joined_out, 'seq', 0, 0, tiled=True).transpose(1, 2, 0, 3)  29.8 us
    dot_general x10, matrix products, bf16_dot(): lax.dot_general(left, right, (dims, ((), ())), preferred_element_type=jnp...  22.7 us
    all_to_all x1, blocking collectives, local(): moved = lax.all_to_all(chunks, 'seq', 0, 0, tiled=True)  19.2 us
    cos x1, other arithmetic, dft_tables(): table = jnp.concatenate([jnp.cos(angle), -jnp.sin(angle)], axis=0)  16.2 us
    unnamed x25, local copies, waits for them, and re-layouts  9.91 us
    all_to_all x1, waiting for transfers between devices, local(): lax.all_to_all(arranged, 'seq', 0, 0, tiled=True).reshape(length, 5, narrow)  7.21 us
    concatenate x1, other arithmetic, local(): jnp.concatenate([features.reshape(tok_rows, 3 * chan_width), cotangent.re...  5.61 us
    all_to_all x1, starting transfers between devices, local(): lax.all_to_all(arranged, 'seq', 0, 0, tiled=True).reshape(length, 5, narrow)  5.17 us
  transfers between devices with their start and end apart: 2, of which 1 were waited for; matrix products, arithmetic and copies ran while one was open for 22% of the time, Pallas kernels for 0%

profile of v1, /device:TPU:0, one launch (start us, length us, event | category | flops | bytes accessed | tf_op | source)
XLA Modules:
  0.0 158.1 jit_solution(269031285280743898)
XLA Ops:
  7.2 2.7 %copy.33 = bf16[1,128,6144]{1,2,0:T(8,128)(2,1)} copy(bf16[1,128,6144]{2,1,0:T(8,128)(2,1)} %param.5) | data formatting | bytes 3145728 | tf_op args[0]
  9.9 0.3 copy.34
  10.1 1.0 copy.35
  11.1 5.6 %pad_maximum_fusion.4 = bf16[128,10240]{0,1:T(8,128)(2,1)S(1)} fusion(bf16[128,2048]{0,1:T(8,128)(2,1)} %copy.35, bf16[128,2048]{0,1:T(8,128)(2,1)S(1)} %bitcast.104, bf16[128,6144]{0,1:T(8,128)(2,1)} %bitcast.99), kind=kLoop, calls=%fused_computation.33 | loop fusion | flops 7864320 | bytes 5242880 | tf_op jit(solution)/shard_map/concatenate | solution.py:262
  16.8 2.6 %copy.36 = bf16[8,128,5,256]{3,1,2,0:T(8,128)(2,1)} copy(bf16[8,128,5,256]{1,3,0,2:T(8,128)(2,1)S(1)} %bitcast.95) | data formatting | bytes 5242880 | tf_op jit(solution)/shard_map/transpose | solution.py:270
  19.4 5.2 %all-to-all-start = ((bf16[8,128,5,256]{3,1,2,0:T(8,128)(2,1)}), bf16[8,128,5,256]{3,1,2,0:T(8,128)(2,1)S(1)}, u32[]{:S(2)}, u32[]{:S(2)}) async-start(bf16[8,128,5,256]{3,1,2,0:T(8,128)(2,1)} %copy.36), calls=%async_computation | async-start | bytes 5242880 | tf_op jit(solution)/shard_map/all_to_all | solution.py:271
  24.6 3.7 %add_select_fusion = s32[1025,1024]{1,0:T(8,128)} fusion(), kind=kLoop, calls=%fused_computation.3 | loop fusion | flops 12595200 | bytes 4198400 | tf_op jit(solution)/shard_map/jit(remainder)/select_n | solution.py:129
  28.3 0.1 reshape.90
  28.4 0.8 dynamic_slice.7
  29.3 16.2 %fusion.7 = (f32[1025,1024]{1,0:T(8,128)S(1)}, f32[1025,1024]{1,0:T(8,128)S(1)}) fusion(s32[1025,1024]{1,0:T(8,128)} %add_select_fusion), kind=kLoop, calls=%fused_computation.19 | loop fusion | flops 3148800 | bytes 12595200 | tf_op jit(solution)/shard_map/cos | solution.py:132
  45.5 4.2 %subtract_convert_fusion = (bf16[2050,1024]{1,0:T(8,128)(2,1)}, bf16[2050,1024]{1,0:T(8,128)(2,1)}) fusion(f32[1025,1024]{1,0:T(8,128)S(1)} %get-tuple-element.25, f32[1025,1024]{1,0:T(8,128)S(1)} %get-tuple-element.24), kind=kLoop, calls=%fused_computation.1 | loop fusion | flops 16793600 | bytes 16793600 | tf_op jit(solution)/shard_map/convert_element_type | solution.py:134
  49.6 7.2 %all-to-all-done = bf16[8,128,5,256]{3,1,2,0:T(8,128)(2,1)S(1)} async-done(((bf16[8,128,5,256]{3,1,2,0:T(8,128)(2,1)}), bf16[8,128,5,256]{3,1,2,0:T(8,128)(2,1)S(1)}, u32[]{:S(2)}, u32[]{:S(2)}) %all-to-all-start) | async-done | bytes 2621472 | tf_op jit(solution)/shard_map/all_to_all | solution.py:271
  56.8 0.2 copy.37
  57.0 0.1 slice.129
  57.2 1.0 fusion.9
  58.2 0.4 fusion.20
  58.6 0.7 slice-done.2
  59.3 2.4 %fusion.23 = f32[2050,512]{1,0:T(8,128)S(1)} fusion(bf16[2050,1024]{1,0:T(8,128)(2,1)S(1)} %bitcast.102, bf16[1024,256]{1,0:T(8,128)(2,1)S(1)} %slice_bitcast_fusion.4, bf16[1024,256]{1,0:T(8,128)(2,1)S(1)} %get-tuple-element.14), kind=kOutput, calls=%fused_computation.73 | convolution fusion | flops 2151677952 | bytes 9445376 | tf_op jit(solution)/shard_map/dot_general | solution.py:139
  61.8 2.6 %convolution_add_fusion = f32[2050,512]{1,0:T(8,128)S(1)} fusion(f32[2050,512]{1,0:T(8,128)S(1)} %fusion.23, bf16[2050,1024]{1,0:T(8,128)(2,1)S(1)} %bitcast.89, bf16[1024,256]{1,0:T(8,128)(2,1)S(1)} %slice_bitcast_fusion.4, bf16[1024,256]{1,0:T(8,128)(2,1)S(1)} %get-tuple-element.14), kind=kOutput, calls=%fused_computation.6 | convolution fusion | flops 2152727552 | bytes 13643776 | tf_op jit(solution)/shard_map/dot_general | solution.py:139
  64.4 0.3 multiply_subtract_fusion.2
  64.8 1.4 fusion.43
  66.2 1.5 convolution_add_fusion.1
  67.7 0.7 multiply_add_fusion.1
  68.4 2.8 %fusion.39 = f32[1024,512]{1,0:T(8,128)S(1)} fusion(bf16[2050,1024]{1,0:T(8,128)(2,1)S(1)} %bitcast.102, f32[1025,256]{1,0:T(8,128)S(1)} %get-tuple-element.20, f32[1025,256]{1,0:T(8,128)S(1)} %get-tuple-element.19, f32[1025,256]{1,0:T(8,128)S(1)} %get-tuple-element.21, f32[1025,256]{1,0:T(8,128)S(1)} %get-tuple-element.18, f32[2050]{0:T(1024)S(1)} %fusion.27), kind=kOutput, calls=%fused_computation.96 | convolution fusion | flops 2154828800 | bytes 10502152 | tf_op jit(solution)/shard_map/dot_general | solution.py:139
  71.2 3.0 %fusion.36 = f32[1024,512]{1,0:T(8,128)S(1)} fusion(bf16[2050,1024]{1,0:T(8,128)(2,1)S(1)} %bitcast.89, f32[1025,256]{1,0:T(8,128)S(1)} %get-tuple-element.20, f32[1025,256]{1,0:T(8,128)S(1)} %get-tuple-element.19, f32[1025,256]{1,0:T(8,128)S(1)} %get-tuple-element.21, f32[1025,256]{1,0:T(8,128)S(1)} %get-tuple-element.18, f32[2050]{0:T(1024)S(1)} %fusion.27), kind=kOutput, calls=%fused_computation.95 | convolution fusion | flops 2154828800 | bytes 10502152 | tf_op jit(solution)/shard_map/dot_general | solution.py:139
  74.2 2.0 %fusion.34 = f32[1024,256]{1,0:T(8,128)S(1)} fusion(bf16[2050,1024]{1,0:T(8,128)(2,1)S(1)} %bitcast.102, f32[1025,256]{1,0:T(8,128)S(1)} %get-tuple-element.27, f32[1025,256]{1,0:T(8,128)S(1)} %get-tuple-element.26, f32[2050]{0:T(1024)S(1)} %fusion.27), kind=kOutput, calls=%fused_computation.94 | convolution fusion | flops 1076364800 | bytes 7354376 | tf_op jit(solution)/shard_map/dot_general | solution.py:139
  76.2 2.0 %convolution_add_fusion.3 = f32[1024,256]{1,0:T(8,128)S(1)} fusion(f32[1024,256]{1,0:T(8,128)S(1)} %fusion.34, bf16[2050,1024]{1,0:T(8,128)(2,1)S(1)} %bitcast.102, f32[1025,256]{1,0:T(8,128)S(1)} %get-tuple-element.27, f32[1025,256]{1,0:T(8,128)S(1)} %get-tuple-element.26, f32[2050]{0:T(1024)S(1)} %fusion.27), kind=kOutput, calls=%fused_computation.51 | convolution fusion | flops 1078201344 | bytes 8402952 | tf_op jit(solution)/shard_map/dot_general | solution.py:139
  78.2 2.1 %fusion.17 = f32[1024,256]{1,0:T(8,128)S(1)} fusion(f32[1024,256]{1,0:T(8,128)S(1)} %convolution_add_fusion.3, bf16[2050,1024]{1,0:T(8,128)(2,1)S(1)} %bitcast.89, bf16[1024,256]{1,0:T(8,128)(2,1)S(1)} %get-tuple-element.14, f32[256]{0:T(256)S(1)} %dynamic_slice.7, f32[1025,256]{1,0:T(8,128)S(1)} %get-tuple-element.27, ...), kind=kOutput, calls=%fused_computation.52 | convolution fusion | flops 1077413376 | bytes 8928264 | tf_op jit(solution)/shard_map/dot_general | solution.py:139
  80.3 0.1 fusion.21
  80.4 2.8 %add_add_fusion = f32[1024,512]{1,0:T(8,128)S(1)} fusion(f32[1024,512]{1,0:T(8,128)S(1)} %fusion.36, f32[1024,512]{1,0:T(8,128)S(1)} %fusion.39, bf16[2050,1024]{1,0:T(8,128)(2,1)S(1)} %bitcast.102, f32[1025,256]{1,0:T(8,128)S(1)} %get-tuple-element.20, f32[1025,256]{1,0:T(8,128)S(1)} %get-tuple-element.19, f32[1025,256]{1,0:T(8,128)S(1)} %get-tuple-element.21, ...), kind=kOutput, calls=%fused_computation.40 | convolution fusion | flops 2159026176 | bytes 14696456 | tf_op jit(solution)/shard_map/dot_general | solution.py:139
  83.2 1.5 multiply_bitcast_fusion.1
  84.7 1.3 fusion.11
  86.2 1.3 pad_maximum_fusion.7
  87.5 19.2 %all_to_all.15 = f32[8,144,256]{2,1,0:T(8,128)S(1)} all-to-all(f32[8,144,256]{2,1,0:T(8,128)S(1)} %pad_maximum_fusion.7), channel_id=1, replica_groups=mesh['dp'=4,'seq'=8] {'seq'}, dimensions={0} | all-to-all | bytes 2359296 | tf_op jit(solution)/shard_map/all_to_all | solution.py:303
  106.8 1.2 pad_maximum_fusion.6
  108.1 1.0 add_convert_fusion
  109.1 0.2 pad_maximum_fusion.5
  109.3 29.8 %all_to_all.16 = bf16[8,128,4,256]{3,1,2,0:T(8,128)(2,1)} all-to-all(bf16[8,128,4,256]{3,1,2,0:T(8,128)(2,1)S(1)} %pad_maximum_fusion.5), channel_id=1, replica_groups=mesh['dp'=4,'seq'=8] {'seq'}, dimensions={0} | all-to-all | bytes 4194304 | tf_op jit(solution)/shard_map/all_to_all | solution.py:288
  139.1 3.0 %copy.40 = bf16[8,128,4,256]{1,3,0,2:T(8,128)(2,1)S(1)} copy(bf16[8,128,4,256]{3,1,2,0:T(8,128)(2,1)} %all_to_all.16) | data formatting | bytes 4194304 | tf_op jit(solution)/shard_map/all_to_all | solution.py:288
  142.1 1.3 slice.143
  143.4 2.6 %copy.47 = bf16[1,128,6144]{2,1,0:T(8,128)(2,1)} copy(bf16[1,128,6144]{1,2,0:T(8,128)(2,1)} %bitcast.98) | data formatting | bytes 3145728
  146.0 1.0 copy.46
  147.0 0.9 slice.147
  148.0 1.0 slice.150
  149.0 0.1 copy.49
  149.1 0.8 copy.48
  149.9 0.7 reshape.102
  150.7 0.6 copy.50
  (39 shorter events, 0.6 us)
Async XLA Ops:
  7.2 2.7 %copy-start.1 = (bf16[1,128,2048]{2,1,0:T(8,128)(2,1)S(1)}, bf16[1,128,2048]{2,1,0:T(8,128)(2,1)}, u32[]{:S(2)}) copy-start(bf16[1,128,2048]{2,1,0:T(8,128)(2,1)} %param.9) | copy-start | bytes 1572868
  7.2 3.0 %copy-start.2 = (bf16[128,2048]{1,0:T(8,128)(2,1)S(1)}, bf16[128,2048]{1,0:T(8,128)(2,1)}, u32[]{:S(2)}) copy-start(bf16[128,2048]{1,0:T(8,128)(2,1)} %param.7) | copy-start | bytes 1572868
  19.4 37.4 %all-to-all-start = ((bf16[8,128,5,256]{3,1,2,0:T(8,128)(2,1)}), bf16[8,128,5,256]{3,1,2,0:T(8,128)(2,1)S(1)}, u32[]{:S(2)}, u32[]{:S(2)}) async-start(bf16[8,128,5,256]{3,1,2,0:T(8,128)(2,1)} %copy.36), calls=%async_computation | async-start | bytes 5242880 | tf_op jit(solution)/shard_map/all_to_all | solution.py:271
  24.6 3.8 %copy-start.3 = (f32[3,6144]{1,0:T(4,128)S(1)}, f32[3,6144]{1,0:T(4,128)}, u32[]{:S(2)}) copy-start(f32[3,6144]{1,0:T(4,128)} %param.6) | copy-start | bytes 221188
  24.6 122.4 %reduce-scatter.2.cloned.1.call-start = ((), (), s32[]{:S(2)}) async-start(), calls=%async_computation.4 | async-start | bytes 1720320 | tf_op jit(solution)/shard_map/reduce_scatter | solution.py:314
  57.1 2.2 %slice-start.2 = ((s8[4210688]{0:T(1024)(128)(4,1)}), s8[4194304]{0:T(1024)(128)(4,1)S(1)}, s32[]{:S(2)}) async-start(s8[4210688]{0:T(1024)(128)(4,1)} %bitcast.101), calls=%async_computation.7 | async-start | bytes 8388608
  57.2 2.1 %slice-start.3 = ((s8[4210688]{0:T(1024)(128)(4,1)}), s8[16384]{0:T(1024)(128)(4,1)S(1)}, s32[]{:S(2)}) async-start(s8[4210688]{0:T(1024)(128)(4,1)} %bitcast.101), calls=%async_computation.8 | async-start | bytes 32768
  58.2 3.6 %slice-start = ((s8[4210688]{0:T(1024)(128)(4,1)}), s8[4194304]{0:T(1024)(128)(4,1)S(1)}, s32[]{:S(2)}) async-start(s8[4210688]{0:T(1024)(128)(4,1)} %bitcast.88), calls=%async_computation.5 | async-start | bytes 8388608
  59.3 2.5 %slice-start.1 = ((s8[4210688]{0:T(1024)(128)(4,1)}), s8[16384]{0:T(1024)(128)(4,1)S(1)}, s32[]{:S(2)}) async-start(s8[4210688]{0:T(1024)(128)(4,1)} %bitcast.88), calls=%async_computation.6 | async-start | bytes 32768
  108.0 1.0 copy-start
Sparse Core Ops, SparseCore 0:
  108.2 31.6 reduce-scatter.1

commit v2 on v1

--- a/solution.py
+++ b/solution.py
@@ -130,24 +130,19 @@
         2.0 * math.pi / fft_length
     )
     table = jnp.concatenate([jnp.cos(angle), -jnp.sin(angle)], axis=0)
-    high = table.astype(jnp.bfloat16)
-    low = (table - high.astype(jnp.float32)).astype(jnp.bfloat16)
-    return high, low
+    return table.astype(jnp.bfloat16)
 
 
 def bf16_dot(left, right, dims):
     return lax.dot_general(left, right, (dims, ((), ())), preferred_element_type=jnp.float32)
 
 
-def to_spectrum(tables, signal):
-    high, low = tables
-    forward = ((1,), (0,))
-    return bf16_dot(high, signal, forward) + bf16_dot(low, signal, forward)
-
-
-def to_signal(tables, spectrum):
-    high, low = tables
-    bins = high.shape[0] // 2
+def to_spectrum(table, signal):
+    return bf16_dot(table, signal, ((1,), (0,)))
+
+
+def to_signal(table, spectrum):
+    bins = table.shape[0] // 2
     fft_length = 2 * (bins - 1)
     row = lax.broadcasted_iota(jnp.int32, (2 * bins, 1), 0)
     edge = (row == 0) | (row == bins - 1) | (row == bins) | (row == 2 * bins - 1)
@@ -156,11 +151,7 @@
     spec_high = scaled.astype(jnp.bfloat16)
     spec_low = (scaled - spec_high.astype(jnp.float32)).astype(jnp.bfloat16)
     backward = ((0,), (0,))
-    return (
-        bf16_dot(high, spec_high, backward)
-        + bf16_dot(high, spec_low, backward)
-        + bf16_dot(low, spec_high, backward)
-    )
+    return bf16_dot(table, spec_high, backward) + bf16_dot(table, spec_low, backward)
 
 
 def split(spectrum):

time: 159 us -> 154 us (0.969)
  matrix products: 22.7 us -> 13.8 us
  waiting for transfers between devices: 7.23 us -> 9.82 us
  local copies, waits for them, and re-layouts: 21 us -> 23.2 us
    another operation x0 -> x1, other arithmetic: none -> 17.8 us
    cos x1 -> x0, other arithmetic: 16.2 us -> none  [dft_tables(): table = jnp.concatenate([jnp.cos(angle), -jnp.sin(angle)], axis=0)]
    dot_general x10 -> x6, matrix products: 22.7 us -> 13.8 us  [bf16_dot(): lax.dot_general(left, right, (dims, ((), ())), preferred_element_type=jnp...]
    convert_element_type x1 -> x0, other arithmetic: 4.17 us -> none  [dft_tables(): low = (table - high.astype(jnp.float32)).astype(jnp.bfloat16)]
    all_to_all x1, waiting for transfers between devices: 7.21 us -> 9.8 us  [local(): lax.all_to_all(arranged, 'seq', 0, 0, tiled=True).reshape(length, 5, narrow)]
    unnamed x25 -> x19, local copies, waits for them, and re-layouts: 9.91 us -> 12.1 us
  transfers between devices with their start and end apart: 2 -> 2, of which waited for: 1 -> 1; matrix products, arithmetic and copies ran while one was open for 22% -> 21% of each run, Pallas kernels for 0% -> 0%
where the time goes in v2:
time: 154 us; the launch traced here: 153 us
  blocking collectives  48.9 us (32%)
  other arithmetic  37.6 us (24%)
  local copies, waits for them, and re-layouts  23.2 us (15%)
  between operations  14.3 us (9%)
  matrix products  13.8 us (9%)
  waiting for transfers between devices  9.82 us (6%)
  starting transfers between devices  5.34 us (3%)
    all_to_all x1, blocking collectives, local(): lax.all_to_all(joined_out, 'seq', 0, 0, tiled=True).transpose(1, 2, 0, 3)  29.7 us
    all_to_all x1, blocking collectives, local(): moved = lax.all_to_all(chunks, 'seq', 0, 0, tiled=True)  19.2 us
    another operation x1, other arithmetic  17.8 us
    dot_general x6, matrix products, bf16_dot(): lax.dot_general(left, right, (dims, ((), ())), preferred_element_type=jnp...  13.8 us
    unnamed x19, local copies, waits for them, and re-layouts  12.1 us
    all_to_all x1, waiting for transfers between devices, local(): lax.all_to_all(arranged, 'seq', 0, 0, tiled=True).reshape(length, 5, narrow)  9.8 us
    concatenate x1, other arithmetic, local(): jnp.concatenate([features.reshape(tok_rows, 3 * chan_width), cotangent.re...  6.96 us
    all_to_all x1, starting transfers between devices, local(): lax.all_to_all(arranged, 'seq', 0, 0, tiled=True).reshape(length, 5, narrow)  5.3 us
  transfers between devices with their start and end apart: 2, of which 1 were waited for; matrix products, arithmetic and copies ran while one was open for 21% of the time, Pallas kernels for 0%

profile of v2, /device:TPU:0, one launch (start us, length us, event | category | flops | bytes accessed | tf_op | source)
XLA Modules:
  0.0 153.1 jit_solution(13491635884078304516)
XLA Ops:
  7.2 1.4 copy.35
  8.6 2.0 %copy.34 = bf16[1,128,2048]{1,2,0:T(8,128)(2,1)} copy(bf16[1,128,2048]{2,1,0:T(8,128)(2,1)} %param.9) | data formatting | bytes 1048576 | tf_op args[4]
  10.7 1.6 %copy.33 = bf16[1,128,6144]{1,2,0:T(8,128)(2,1)} copy(bf16[1,128,6144]{2,1,0:T(8,128)(2,1)S(1)} %copy-done.3) | data formatting | bytes 3145728 | tf_op args[0]
  12.2 7.0 %pad_maximum_fusion.4 = bf16[128,10240]{0,1:T(8,128)(2,1)S(1)} fusion(bf16[128,2048]{0,1:T(8,128)(2,1)S(1)} %copy.35, bf16[128,2048]{0,1:T(8,128)(2,1)} %bitcast.89, bf16[128,6144]{0,1:T(8,128)(2,1)} %bitcast.86), kind=kLoop, calls=%fused_computation.29 | loop fusion | flops 7864320 | bytes 5242880 | tf_op jit(solution)/shard_map/concatenate | solution.py:253
  19.2 2.6 %copy.36 = bf16[8,128,5,256]{3,1,2,0:T(8,128)(2,1)} copy(bf16[8,128,5,256]{1,3,0,2:T(8,128)(2,1)S(1)} %bitcast.82) | data formatting | bytes 5242880 | tf_op jit(solution)/shard_map/transpose | solution.py:261
  21.8 5.3 %all-to-all-start = ((bf16[8,128,5,256]{3,1,2,0:T(8,128)(2,1)}), bf16[8,128,5,256]{3,1,2,0:T(8,128)(2,1)S(1)}, u32[]{:S(2)}, u32[]{:S(2)}) async-start(bf16[8,128,5,256]{3,1,2,0:T(8,128)(2,1)} %copy.36), calls=%async_computation | async-start | bytes 5242880 | tf_op jit(solution)/shard_map/all_to_all | solution.py:262
  27.1 0.1 reshape.90
  27.2 3.7 %add_select_fusion = s32[1025,1024]{1,0:T(8,128)} fusion(), kind=kLoop, calls=%fused_computation | loop fusion | flops 12595200 | bytes 4198400 | tf_op jit(solution)/shard_map/jit(remainder)/select_n | solution.py:129
  30.9 0.8 dynamic_slice.7
  31.7 0.1 pad.8.clone
  31.8 17.8 %cosine_convert_fusion = (bf16[1025,1024]{1,0:T(8,128)(2,1)}, bf16[1025,1024]{1,0:T(8,128)(2,1)}) fusion(s32[1025,1024]{1,0:T(8,128)} %add_select_fusion), kind=kLoop, calls=%fused_computation.5 | loop fusion | flops 5248000 | bytes 8396800 | tf_op jit(solution)/shard_map/convert.1
  49.5 9.8 %all-to-all-done = bf16[8,128,5,256]{3,1,2,0:T(8,128)(2,1)S(1)} async-done(((bf16[8,128,5,256]{3,1,2,0:T(8,128)(2,1)}), bf16[8,128,5,256]{3,1,2,0:T(8,128)(2,1)S(1)}, u32[]{:S(2)}, u32[]{:S(2)}) %all-to-all-start) | async-done | bytes 2621472 | tf_op jit(solution)/shard_map/all_to_all | solution.py:262
  59.3 0.3 copy.37
  59.6 0.1 slice.129
  59.8 1.0 fusion.7
  60.8 0.3 fusion.22
  61.2 1.2 copy-done
  62.4 0.6 copy-done.1
  63.0 1.4 fusion.41
  64.5 2.5 %fusion.25 = f32[2050,512]{1,0:T(8,128)S(1)} fusion(bf16[1024,256]{1,0:T(8,128)(2,1)S(1)} %slice_bitcast_fusion.4, bf16[1024,256]{1,0:T(8,128)(2,1)S(1)} %get-tuple-element.14, bf16[1025,1024]{1,0:T(8,128)(2,1)S(1)} %copy-done.1, bf16[1025,1024]{1,0:T(8,128)(2,1)S(1)} %copy-done), kind=kOutput, calls=%fused_computation.65 | convolution fusion | flops 2160074752 | bytes 9445376 | tf_op jit(solution)/shard_map/dot_general | solution.py:137
  66.9 0.3 multiply_subtract_fusion.2
  67.3 0.7 multiply_add_fusion.1
  67.9 2.8 %fusion.30 = f32[1024,512]{1,0:T(8,128)S(1)} fusion(f32[1025,256]{1,0:T(8,128)S(1)} %get-tuple-element.18, f32[1025,256]{1,0:T(8,128)S(1)} %get-tuple-element.17, f32[1025,256]{1,0:T(8,128)S(1)} %get-tuple-element.19, f32[1025,256]{1,0:T(8,128)S(1)} %get-tuple-element.16, f32[2050]{0:T(1024)S(1)} %fusion.35, bf16[1025,1024]{1,0:T(8,128)(2,1)S(1)} %copy-done.1, ...), kind=kOutput, calls=%fused_computation.75 | convolution fusion | flops 2163225600 | bytes 10502152 | tf_op jit(solution)/shard_map/dot_general | solution.py:137
  70.7 2.8 %fusion.15 = f32[1024,512]{1,0:T(8,128)S(1)} fusion(f32[1024,512]{1,0:T(8,128)S(1)} %fusion.30, f32[1025,256]{1,0:T(8,128)S(1)} %get-tuple-element.18, f32[1025,256]{1,0:T(8,128)S(1)} %get-tuple-element.17, f32[1025,256]{1,0:T(8,128)S(1)} %get-tuple-element.19, f32[1025,256]{1,0:T(8,128)S(1)} %get-tuple-element.16, f32[2050]{0:T(1024)S(1)} %fusion.35, ...), kind=kOutput, calls=%fused_computation.37 | convolution fusion | flops 2166898688 | bytes 12599304 | tf_op jit(solution)/shard_map/dot_general | solution.py:137
  73.6 2.2 %fusion.17 = f32[1024,256]{1,0:T(8,128)S(1)} fusion(f32[1025,256]{1,0:T(8,128)S(1)} %get-tuple-element.25, f32[1025,256]{1,0:T(8,128)S(1)} %get-tuple-element.24, f32[2050]{0:T(1024)S(1)} %fusion.35, bf16[1025,1024]{1,0:T(8,128)(2,1)S(1)} %copy-done.1, bf16[1025,1024]{1,0:T(8,128)(2,1)S(1)} %copy-done), kind=kOutput, calls=%fused_computation.49 | convolution fusion | flops 1084761600 | bytes 7354376 | tf_op jit(solution)/shard_map/dot_general | solution.py:137
  75.9 2.1 %fusion.16 = f32[1024,256]{1,0:T(8,128)S(1)} fusion(f32[1024,256]{1,0:T(8,128)S(1)} %fusion.17, f32[1025,256]{1,0:T(8,128)S(1)} %get-tuple-element.25, f32[1025,256]{1,0:T(8,128)S(1)} %get-tuple-element.24, f32[2050]{0:T(1024)S(1)} %fusion.35, bf16[1024,256]{1,0:T(8,128)(2,1)S(1)} %get-tuple-element.14, f32[256]{0:T(256)S(1)} %dynamic_slice.7, ...), kind=kOutput, calls=%fused_computation.47 | convolution fusion | flops 1087384576 | bytes 8928264 | tf_op jit(solution)/shard_map/dot_general | solution.py:137
  77.9 0.2 fusion.23
  78.1 1.6 %multiply_bitcast_fusion.1 = (f32[1024,1,256]{2,0,1:T(8,128)S(1)}, f32[1024,1,256]{2,0,1:T(8,128)S(1)}, bf16[1024,256]{1,0:T(8,128)(2,1)}, f32[1024,256]{1,0:T(8,128)}) fusion(f32[1024,3,256]{2,0,1:T(8,128)S(1)} %fusion.7, bf16[1024,256]{1,0:T(8,128)(2,1)S(1)} %get-tuple-element.15, f32[1024,512]{1,0:T(8,128)S(1)} %fusion.15, f32[256]{0:T(256)S(1)} %dynamic_slice.7, ...), kind=kLoop, calls=%fused_computation.70 | loop fusion | flops 1835008 | bytes 10486784 | tf_op jit(solution)/shard_map/stack | solution.py:191
  79.7 1.3 fusion.9
  81.0 0.1 maximum_maximum_fusion
  81.1 1.3 pad_maximum_fusion.7
  82.4 19.2 %all_to_all.15 = f32[8,144,256]{2,1,0:T(8,128)S(1)} all-to-all(f32[8,144,256]{2,1,0:T(8,128)S(1)} %pad_maximum_fusion.7), channel_id=1, replica_groups=mesh['dp'=4,'seq'=8] {'seq'}, dimensions={0} | all-to-all | bytes 2359296 | tf_op jit(solution)/shard_map/all_to_all | solution.py:294
  101.6 0.1 copy.41
  101.7 0.1 slice.145
  101.8 1.2 pad_maximum_fusion.6
  103.0 1.0 add_convert_fusion
  104.1 0.2 pad_maximum_fusion.5
  104.3 29.7 %all_to_all.16 = bf16[8,128,4,256]{3,1,2,0:T(8,128)(2,1)} all-to-all(bf16[8,128,4,256]{3,1,2,0:T(8,128)(2,1)S(1)} %pad_maximum_fusion.5), channel_id=1, replica_groups=mesh['dp'=4,'seq'=8] {'seq'}, dimensions={0} | all-to-all | bytes 4194304 | tf_op jit(solution)/shard_map/all_to_all | solution.py:279
  134.0 3.0 %copy.40 = bf16[8,128,4,256]{1,3,0,2:T(8,128)(2,1)S(1)} copy(bf16[8,128,4,256]{3,1,2,0:T(8,128)(2,1)} %all_to_all.16) | data formatting | bytes 4194304 | tf_op jit(solution)/shard_map/all_to_all | solution.py:279
  137.1 1.3 slice.143
  138.4 1.0 copy.46
  139.4 2.6 %copy.47 = bf16[1,128,6144]{2,1,0:T(8,128)(2,1)} copy(bf16[1,128,6144]{1,2,0:T(8,128)(2,1)} %bitcast.85) | data formatting | bytes 3145728
  142.0 0.9 slice.147
  143.0 0.7 reshape.102
  143.7 0.6 copy.50
  144.3 1.0 slice.150
  145.3 0.1 copy.49
  145.4 0.8 copy.48
  (26 shorter events, 0.3 us)
Async XLA Ops:
  7.2 3.5 %copy-start.3 = (bf16[1,128,6144]{2,1,0:T(8,128)(2,1)S(1)}, bf16[1,128,6144]{2,1,0:T(8,128)(2,1)}, u32[]{:S(2)}) copy-start(bf16[1,128,6144]{2,1,0:T(8,128)(2,1)} %param.5) | copy-start | bytes 4718596
  21.8 5.4 %copy-start.4 = (f32[3,6144]{1,0:T(4,128)S(1)}, f32[3,6144]{1,0:T(4,128)}, u32[]{:S(2)}) copy-start(f32[3,6144]{1,0:T(4,128)} %param.6) | copy-start | bytes 221188
  21.8 37.6 %all-to-all-start = ((bf16[8,128,5,256]{3,1,2,0:T(8,128)(2,1)}), bf16[8,128,5,256]{3,1,2,0:T(8,128)(2,1)S(1)}, u32[]{:S(2)}, u32[]{:S(2)}) async-start(bf16[8,128,5,256]{3,1,2,0:T(8,128)(2,1)} %copy.36), calls=%async_computation | async-start | bytes 5242880 | tf_op jit(solution)/shard_map/all_to_all | solution.py:262
  27.1 114.9 %reduce-scatter.2.cloned.1.call-start = ((), (), s32[]{:S(2)}) async-start(), calls=%async_computation.4 | async-start | bytes 1720320 | tf_op jit(solution)/shard_map/reduce_scatter | solution.py:305
  60.8 1.6 %copy-start = (bf16[1025,1024]{1,0:T(8,128)(2,1)S(1)}, bf16[1025,1024]{1,0:T(8,128)(2,1)}, u32[]{:S(2)}) copy-start(bf16[1025,1024]{1,0:T(8,128)(2,1)} %get-tuple-element.22) | copy-start | bytes 6297604
  60.8 2.2 %copy-start.1 = (bf16[1025,1024]{1,0:T(8,128)(2,1)S(1)}, bf16[1025,1024]{1,0:T(8,128)(2,1)}, u32[]{:S(2)}) copy-start(bf16[1025,1024]{1,0:T(8,128)(2,1)} %get-tuple-element.23) | copy-start | bytes 6297604
  103.0 1.0 copy-start.2
Sparse Core Ops, SparseCore 0:
  103.1 31.6 reduce-scatter.1

commit v3 on v2

--- a/solution.py
+++ b/solution.py
@@ -163,7 +163,7 @@
     return jnp.concatenate([real, imag], axis=0)
 
 
-def block_core(feats, cot, resp, taps, skip_gain):
+def block_core(feats, cot, resp, taps, skip_gain, gated_exchange):
     length = feats.shape[0]
     narrow = feats.shape[2]
     tables = dft_tables(length)
@@ -183,9 +183,11 @@
     gated = (query_feat * carried).astype(jnp.bfloat16)
     grad_carried = (cot * query_feat).astype(jnp.bfloat16)
     grad_query = cot * carried
+    gated_moved = gated_exchange(gated)
     grad_re, grad_im = split(to_spectrum(tables, grad_carried))
     back_spec = join(grad_re * resp_re + grad_im * resp_im, grad_im * resp_re - grad_re * resp_im)
     filt_spec = join(grad_re * prod_re + grad_im * prod_im, grad_im * prod_re - grad_re * prod_im)
+    back_spec, gated_moved = lax.optimization_barrier((back_spec, gated_moved))
     both = to_signal(tables, jnp.concatenate([back_spec, filt_spec], axis=1))
     grad_product = both[:, :narrow] + skip_gain * grad_carried
     grad_mixed = jnp.stack([grad_query, grad_product * value_feat, grad_product * key_feat], axis=1)
@@ -200,7 +202,7 @@
         ]
     )
     grad_skip = jnp.sum(grad_carried.astype(jnp.float32) * product.astype(jnp.float32), axis=0)
-    return gated, grad_feats, grad_taps, grad_skip, both[:, narrow:]
+    return gated_moved, grad_feats, grad_taps, grad_skip, both[:, narrow:]
 
 
 def blocked_fallback(moved_in, taps, skip_gain, seq_parts, tok_rows, narrow):
@@ -262,23 +264,23 @@
     moved_in = lax.all_to_all(arranged, "seq", 0, 0, tiled=True).reshape(length, 5, narrow)
     local_taps = lax.dynamic_slice_in_dim(taps, offset, narrow, 2)
     local_skip = lax.dynamic_slice_in_dim(skip_gain, offset, narrow, 0)
+    def gated_exchange(gated):
+        return lax.all_to_all(gated.reshape(seq_parts, tok_rows, narrow), "seq", 0, 0, tiled=True)
+
     if length <= 2048:
         gated, grad_feats, grad_taps, grad_skip, filter_part = block_core(
-            moved_in[:, :3], moved_in[:, 3], moved_in[:, 4], local_taps, local_skip
+            moved_in[:, :3], moved_in[:, 3], moved_in[:, 4], local_taps, local_skip, gated_exchange
         )
     else:
         gated, grad_feats, grad_taps, grad_skip, filter_part = blocked_fallback(
             moved_in, local_taps, local_skip, seq_parts, tok_rows, narrow
         )
-        gated = gated.reshape(length, narrow)
+        gated = gated_exchange(gated.reshape(length, narrow))
         grad_feats = grad_feats.reshape(length, 3, narrow)
-    joined_out = jnp.concatenate(
-        [gated.reshape(seq_parts, tok_rows, 1, narrow), grad_feats.reshape(seq_parts, tok_rows, 3, narrow)],
-        axis=2,
-    )
-    moved_out = lax.all_to_all(joined_out, "seq", 0, 0, tiled=True).transpose(1, 2, 0, 3)
-    gated = moved_out[:, 0]
-    grad_feats = moved_out[:, 1:]
+    gated = gated.transpose(1, 0, 2)
+    grad_feats = lax.all_to_all(
+        grad_feats.reshape(seq_parts, tok_rows, 3, narrow), "seq", 0, 0, tiled=True
+    ).transpose(1, 2, 0, 3)
     extra = 16
     small = jnp.concatenate(
         [grad_taps.reshape(9, narrow), grad_skip[None], jnp.zeros((extra - 10, narrow), jnp.float32)],

time: 154 us -> 169 us (1.097)
  blocking collectives: 48.9 us -> 19.2 us
  waiting for transfers between devices: 9.82 us -> 33.9 us
  starting transfers between devices: 5.34 us -> 13.3 us
  matrix products: 13.8 us -> 19.5 us
  other arithmetic: 37.6 us -> 42.8 us
  local copies, waits for them, and re-layouts: 23.2 us -> 25.2 us
    all_to_all x1 -> x0, blocking collectives: 29.7 us -> none  [local(): lax.all_to_all(joined_out, 'seq', 0, 0, tiled=True).transpose(1, 2, 0, 3)]
    all_to_all x0 -> x2, waiting for transfers between devices: none -> 21.7 us  [the longest x1 18.6 us: local(): lax.all_to_all(grad_feats.reshape(seq_parts, tok_rows, 3, narrow), 'seq',...]
    all_to_all x0 -> x2, starting transfers between devices: none -> 7.72 us  [the longest x1 4.14 us: gated_exchange(): lax.all_to_all(gated.reshape(seq_parts, tok_rows, narrow), 'seq', 0, 0, t...]
    dot_general x6, matrix products: 13.8 us -> 19.5 us  [bf16_dot(): lax.dot_general(left, right, (dims, ((), ())), preferred_element_type=jnp...]
    add x1, other arithmetic: 0.65 us -> 4.79 us  [block_core(): grad_re * prod_re + grad_im * prod_im]
    reduce_scatter x1, waiting for transfers between devices: 0.01 us -> 2.49 us  [local(): reduced = lax.psum_scatter(joined, 'dp', scatter_dimension=0, tiled=True)]
    reshape x0 -> x2, local copies, waits for them, and re-layouts: none -> 2.29 us  [the longest x1 1.25 us: local(): grad_feats.reshape(seq_parts, tok_rows, 3, narrow)]
    all_to_all x1, local copies, waits for them, and re-layouts: 3.04 us -> 0.89 us  [local(): lax.all_to_all(grad_feats.reshape(seq_parts, tok_rows, 3, narrow), 'seq',...]
  transfers between devices with their start and end apart: 2 -> 4, of which waited for: 1 -> 4; matrix products, arithmetic and copies ran while one was open for 21% -> 21% of each run, Pallas kernels for 0% -> 0%
where the time goes in v3:
time: 169 us; the launch traced here: 168 us
  other arithmetic  42.8 us (25%)
  waiting for transfers between devices  33.9 us (20%)
  local copies, waits for them, and re-layouts  25.2 us (15%)
  matrix products  19.5 us (12%)
  blocking collectives  19.2 us (11%)
  between operations  14.4 us (9%)
  starting transfers between devices  13.3 us (8%)
    dot_general x6, matrix products, bf16_dot(): lax.dot_general(left, right, (dims, ((), ())), preferred_element_type=jnp...  19.5 us
    all_to_all x1, blocking collectives, local(): moved = lax.all_to_all(chunks, 'seq', 0, 0, tiled=True)  19.2 us
    all_to_all x1, waiting for transfers between devices, local(): lax.all_to_all(grad_feats.reshape(seq_parts, tok_rows, 3, narrow), 'seq',...  18.6 us
    another operation x1, other arithmetic  17.8 us
    unnamed x42, local copies, waits for them, and re-layouts  13.9 us
    all_to_all x1, waiting for transfers between devices, local(): lax.all_to_all(arranged, 'seq', 0, 0, tiled=True).reshape(length, 5, narrow)  9.71 us
    concatenate x1, other arithmetic, local(): jnp.concatenate([features.reshape(tok_rows, 3 * chan_width), cotangent.re...  6.96 us
    all_to_all x1, starting transfers between devices, local(): lax.all_to_all(arranged, 'seq', 0, 0, tiled=True).reshape(length, 5, narrow)  5.3 us
  transfers between devices with their start and end apart: 4, of which 4 were waited for; matrix products, arithmetic and copies ran while one was open for 21% of the time, Pallas kernels for 0%

profile of v3, /device:TPU:0, one launch (start us, length us, event | category | flops | bytes accessed | tf_op | source)
XLA Modules:
  0.0 168.3 jit_solution(449988545816407504)
XLA Ops:
  7.2 1.4 copy.35
  8.6 2.0 %copy.34 = bf16[1,128,2048]{1,2,0:T(8,128)(2,1)} copy(bf16[1,128,2048]{2,1,0:T(8,128)(2,1)} %param.9) | data formatting | bytes 1048576 | tf_op args[4]
  10.7 1.6 copy.33
  12.2 7.0 %pad_maximum_fusion.3 = bf16[128,10240]{0,1:T(8,128)(2,1)S(1)} fusion(bf16[128,2048]{0,1:T(8,128)(2,1)S(1)} %copy.35, bf16[128,2048]{0,1:T(8,128)(2,1)} %bitcast.86, bf16[128,6144]{0,1:T(8,128)(2,1)} %bitcast.84), kind=kLoop, calls=%fused_computation.29 | loop fusion | flops 7864320 | bytes 5242880 | tf_op jit(solution)/shard_map/concatenate | solution.py:255
  19.2 2.6 %copy.36 = bf16[8,128,5,256]{3,1,2,0:T(8,128)(2,1)} copy(bf16[8,128,5,256]{1,3,0,2:T(8,128)(2,1)S(1)} %bitcast.81) | data formatting | bytes 5242880 | tf_op jit(solution)/shard_map/transpose | solution.py:263
  21.8 5.3 %all-to-all-start = ((bf16[8,128,5,256]{3,1,2,0:T(8,128)(2,1)}), bf16[8,128,5,256]{3,1,2,0:T(8,128)(2,1)S(1)}, u32[]{:S(2)}, u32[]{:S(2)}) async-start(bf16[8,128,5,256]{3,1,2,0:T(8,128)(2,1)} %copy.36), calls=%async_computation | async-start | bytes 5242880 | tf_op jit(solution)/shard_map/all_to_all | solution.py:264
  27.2 3.8 %add_select_fusion = s32[1025,1024]{1,0:T(8,128)} fusion(), kind=kLoop, calls=%fused_computation | loop fusion | flops 12595200 | bytes 4198400 | tf_op jit(solution)/shard_map/jit(remainder)/select_n | solution.py:129
  31.0 0.8 dynamic_slice.7
  31.9 17.8 %cosine_convert_fusion = (bf16[1025,1024]{1,0:T(8,128)(2,1)}, bf16[1025,1024]{1,0:T(8,128)(2,1)}) fusion(s32[1025,1024]{1,0:T(8,128)} %add_select_fusion), kind=kLoop, calls=%fused_computation.5 | loop fusion | flops 5248000 | bytes 8396800 | tf_op jit(solution)/shard_map/convert.1
  49.6 9.7 %all-to-all-done = bf16[8,128,5,256]{3,1,2,0:T(8,128)(2,1)S(1)} async-done(((bf16[8,128,5,256]{3,1,2,0:T(8,128)(2,1)}), bf16[8,128,5,256]{3,1,2,0:T(8,128)(2,1)S(1)}, u32[]{:S(2)}, u32[]{:S(2)}) %all-to-all-start) | async-done | bytes 2621472 | tf_op jit(solution)/shard_map/all_to_all | solution.py:264
  59.8 1.0 fusion.7
  60.8 0.4 copy-done.3
  61.2 0.3 fusion.22
  61.6 1.5 copy-done.5
  63.0 0.6 copy-done.7
  63.6 2.7 %fusion.41 = f32[2050,256]{1,0:T(8,128)} fusion(bf16[1024,256]{1,0:T(8,128)(2,1)S(1)} %get-tuple-element.18, bf16[1025,1024]{1,0:T(8,128)(2,1)S(1)} %copy-done.7, bf16[1025,1024]{1,0:T(8,128)(2,1)S(1)} %copy-done.5), kind=kOutput, calls=%fused_computation.94 | convolution fusion | flops 1083187200 | bytes 6821888 | tf_op jit(solution)/shard_map/dot_general | solution.py:137
  66.3 2.4 %fusion.25 = f32[2050,512]{1,0:T(8,128)S(1)} fusion(bf16[1024,256]{1,0:T(8,128)(2,1)S(1)} %slice_bitcast_fusion.3, bf16[1024,256]{1,0:T(8,128)(2,1)S(1)} %get-tuple-element.19, bf16[1025,1024]{1,0:T(8,128)(2,1)S(1)} %copy-done.7, bf16[1025,1024]{1,0:T(8,128)(2,1)S(1)} %copy-done.5), kind=kOutput, calls=%fused_computation.64 | convolution fusion | flops 2160074752 | bytes 9445376 | tf_op jit(solution)/shard_map/dot_general | solution.py:137
  68.8 0.3 multiply_subtract_fusion.1
  69.1 1.7 %copy-done.2 = f32[2050,512]{1,0:T(8,128)} copy-done((f32[2050,512]{1,0:T(8,128)}, f32[2050,512]{1,0:T(8,128)S(1)}, u32[]{:S(2)}) %copy-start.2) | copy-done | bytes 4198424
  70.8 2.0 %fusion.17 = f32[1024,256]{1,0:T(8,128)S(1)} fusion(f32[1025,256]{1,0:T(8,128)S(1)} %get-tuple-element.29, f32[1025,256]{1,0:T(8,128)S(1)} %get-tuple-element.28, f32[2050]{0:T(1024)S(1)} %fusion.35, bf16[1025,1024]{1,0:T(8,128)(2,1)S(1)} %copy-done.7, bf16[1025,1024]{1,0:T(8,128)(2,1)S(1)} %copy-done.5), kind=kOutput, calls=%fused_computation.48 | convolution fusion | flops 1084761600 | bytes 7354376 | tf_op jit(solution)/shard_map/dot_general | solution.py:137
  72.8 3.2 %fusion.24 = (f32[1024,1,256]{2,0,1:T(8,128)}, bf16[1024,256]{1,0:T(8,128)(2,1)}) fusion(bf16[1024,5,256]{2,0,1:T(8,128)(2,1)S(1)} %bitcast.79, f32[1024,3,256]{2,0,1:T(8,128)S(1)} %fusion.7, bf16[1024,256]{1,0:T(8,128)(2,1)S(1)} %get-tuple-element.19, f32[256]{0:T(256)S(1)} %dynamic_slice.7, f32[1024,256]{1,0:T(8,128)S(1)} %fusion.17, ...), kind=kOutput, calls=%fused_computation.60 | convolution fusion | flops 1088433152 | bytes 11025416 | tf_op jit(solution)/shard_map/dot_general | solution.py:137
  76.1 4.1 %all-to-all-start.1 = ((bf16[8,128,256]{2,1,0:T(8,128)(2,1)}), bf16[8,128,256]{2,1,0:T(8,128)(2,1)}, u32[]{:S(2)}, u32[]{:S(2)}) async-start(bf16[8,128,256]{2,1,0:T(8,128)(2,1)} %bitcast.89), calls=%async_computation.1 | async-start | bytes 1048576 | tf_op jit(solution)/shard_map/all_to_all | solution.py:268
  80.5 4.8 %multiply_add_fusion = (f32[1025,256]{1,0:T(8,128)}, f32[1025,256]{1,0:T(8,128)}, f32[1025,256]{1,0:T(8,128)S(1)}, f32[1025,256]{1,0:T(8,128)S(1)}) fusion(f32[2050,512]{1,0:T(8,128)} %copy-done.2, f32[2050,256]{1,0:T(8,128)} %fusion.41), kind=kLoop, calls=%fused_computation.50 | loop fusion | flops 3148800 | bytes 10496000 | tf_op jit(solution)/shard_map/add | solution.py:189
  85.3 1.6 pad_maximum_fusion.4
  86.8 3.1 %all-to-all-done.1 = bf16[8,128,256]{2,1,0:T(8,128)(2,1)} async-done(((bf16[8,128,256]{2,1,0:T(8,128)(2,1)}), bf16[8,128,256]{2,1,0:T(8,128)(2,1)}, u32[]{:S(2)}, u32[]{:S(2)}) %all-to-all-start.1) | async-done | bytes 524320 | tf_op jit(solution)/shard_map/all_to_all | solution.py:268
  90.0 6.3 %fusion.30 = f32[1024,512]{1,0:T(8,128)S(1)} fusion(f32[1025,256]{1,0:T(8,128)} %get-tuple-element.21, f32[1025,256]{1,0:T(8,128)} %get-tuple-element.20, f32[2050,256]{1,0:T(8,128)} %pad_maximum_fusion.4, f32[2050]{0:T(1024)S(1)} %fusion.35, bf16[1025,1024]{1,0:T(8,128)(2,1)} %get-tuple-element.27, bf16[1025,1024]{1,0:T(8,128)(2,1)} %get-tuple-element.26), kind=kOutput, calls=%fused_computation.72 | convolution fusion | flops 2162176000 | bytes 10502152 | tf_op jit(solution)/shard_map/dot_general | solution.py:137
  96.4 2.8 %fusion.15 = f32[1024,512]{1,0:T(8,128)S(1)} fusion(f32[1024,512]{1,0:T(8,128)S(1)} %fusion.30, f32[1025,256]{1,0:T(8,128)S(1)} %copy-done.14, f32[1025,256]{1,0:T(8,128)S(1)} %copy-done.13, f32[2050,256]{1,0:T(8,128)S(1)} %copy-done.9, f32[2050]{0:T(1024)S(1)} %fusion.35, bf16[1025,1024]{1,0:T(8,128)(2,1)S(1)} %copy-done.8, ...), kind=kOutput, calls=%fused_computation.36 | convolution fusion | flops 2165849088 | bytes 12599304 | tf_op jit(solution)/shard_map/dot_general | solution.py:137
  99.3 1.3 multiply_bitcast_fusion.1
  100.6 0.8 copy-done.1
  101.4 0.5 copy-done.4
  102.1 1.3 fusion.9
  103.5 1.3 pad_maximum_fusion.6
  104.8 19.2 %all_to_all.20 = f32[8,144,256]{2,1,0:T(8,128)S(1)} all-to-all(f32[8,144,256]{2,1,0:T(8,128)S(1)} %pad_maximum_fusion.6), channel_id=1, replica_groups=mesh['dp'=4,'seq'=8] {'seq'}, dimensions={0} | all-to-all | bytes 2359296 | tf_op jit(solution)/shard_map/all_to_all | solution.py:296
  124.2 1.2 pad_maximum_fusion.5
  125.4 1.0 add_convert_fusion
  126.4 1.3 copy.39
  127.6 3.6 %all-to-all-start.2 = ((bf16[8,128,3,256]{3,1,2,0:T(8,128)(2,1)}), bf16[8,128,3,256]{3,1,2,0:T(8,128)(2,1)S(1)}, u32[]{:S(2)}, u32[]{:S(2)}) async-start(bf16[8,128,3,256]{3,1,2,0:T(8,128)(2,1)} %copy.39), calls=%async_computation.2 | async-start | bytes 3145728 | tf_op jit(solution)/shard_map/all_to_all | solution.py:281
  131.2 1.3 copy.38
  132.6 1.0 reshape.99
  133.6 18.6 %all-to-all-done.2 = bf16[8,128,3,256]{3,1,2,0:T(8,128)(2,1)S(1)} async-done(((bf16[8,128,3,256]{3,1,2,0:T(8,128)(2,1)}), bf16[8,128,3,256]{3,1,2,0:T(8,128)(2,1)S(1)}, u32[]{:S(2)}, u32[]{:S(2)}) %all-to-all-start.2) | async-done | bytes 1572896 | tf_op jit(solution)/shard_map/all_to_all | solution.py:281
  152.2 0.9 copy.40
  153.1 1.6 copy.46
  154.7 2.5 %reduce-scatter.2.cloned.1.call-done = f32[2,168,256]{2,1,0:T(8,128)} async-done(((f32[8,168,256]{2,1,0:T(8,128)}), f32[2,168,256]{2,1,0:T(8,128)}) %reduce-scatter.2.cloned.1.call-update) | async-done | bytes 344080 | tf_op jit(solution)/shard_map/reduce_scatter | solution.py:307
  157.2 0.9 slice.137
  158.1 0.7 reshape.106
  158.9 0.6 copy.49
  159.5 1.0 slice.140
  160.6 0.8 copy.47
  (52 shorter events, 1.7 us)
Async XLA Ops:
  7.2 3.5 %copy-start.12 = (bf16[1,128,6144]{2,1,0:T(8,128)(2,1)S(1)}, bf16[1,128,6144]{2,1,0:T(8,128)(2,1)}, u32[]{:S(2)}) copy-start(bf16[1,128,6144]{2,1,0:T(8,128)(2,1)} %param.5) | copy-start | bytes 4718596
  21.8 5.3 %copy-start.16 = (f32[3,6144]{1,0:T(4,128)S(1)}, f32[3,6144]{1,0:T(4,128)}, u32[]{:S(2)}) copy-start(f32[3,6144]{1,0:T(4,128)} %param.6) | copy-start | bytes 221188
  21.8 37.6 %all-to-all-start = ((bf16[8,128,5,256]{3,1,2,0:T(8,128)(2,1)}), bf16[8,128,5,256]{3,1,2,0:T(8,128)(2,1)S(1)}, u32[]{:S(2)}, u32[]{:S(2)}) async-start(bf16[8,128,5,256]{3,1,2,0:T(8,128)(2,1)} %copy.36), calls=%async_computation | async-start | bytes 5242880 | tf_op jit(solution)/shard_map/all_to_all | solution.py:264
  59.6 13.2 %copy-start = (bf16[8,128,5,256]{3,1,0,2:T(8,128)(2,1)}, bf16[8,128,5,256]{3,1,0,2:T(8,128)(2,1)S(1)}, u32[]{:S(2)}) copy-start(bf16[8,128,5,256]{3,1,0,2:T(8,128)(2,1)S(1)} %copy.37) | copy-start | bytes 7864324
  59.8 1.4 copy-start.3
  61.2 1.8 %copy-start.5 = (bf16[1025,1024]{1,0:T(8,128)(2,1)S(1)}, bf16[1025,1024]{1,0:T(8,128)(2,1)}, u32[]{:S(2)}) copy-start(bf16[1025,1024]{1,0:T(8,128)(2,1)} %get-tuple-element.26) | copy-start | bytes 6297604
  61.2 2.4 %copy-start.7 = (bf16[1025,1024]{1,0:T(8,128)(2,1)S(1)}, bf16[1025,1024]{1,0:T(8,128)(2,1)}, u32[]{:S(2)}) copy-start(bf16[1025,1024]{1,0:T(8,128)(2,1)} %get-tuple-element.27) | copy-start | bytes 6297604
  61.6 4.8 %copy-start.10 = (bf16[1024,256]{1,0:T(8,128)(2,1)}, bf16[1024,256]{1,0:T(8,128)(2,1)S(1)}, u32[]{:S(2)}) copy-start(bf16[1024,256]{1,0:T(8,128)(2,1)S(1)} %get-tuple-element.18) | copy-start | bytes 1572868
  68.8 2.0 %copy-start.2 = (f32[2050,512]{1,0:T(8,128)}, f32[2050,512]{1,0:T(8,128)S(1)}, u32[]{:S(2)}) copy-start(f32[2050,512]{1,0:T(8,128)S(1)} %fusion.25) | copy-start | bytes 12595204
  76.1 13.9 %all-to-all-start.1 = ((bf16[8,128,256]{2,1,0:T(8,128)(2,1)}), bf16[8,128,256]{2,1,0:T(8,128)(2,1)}, u32[]{:S(2)}, u32[]{:S(2)}) async-start(bf16[8,128,256]{2,1,0:T(8,128)(2,1)} %bitcast.89), calls=%async_computation.1 | async-start | bytes 1048576 | tf_op jit(solution)/shard_map/all_to_all | solution.py:268
  80.2 76.9 %reduce-scatter.2.cloned.1.call-start = ((), (), s32[]{:S(2)}) async-start(), calls=%async_computation.5 | async-start | bytes 1720320 | tf_op jit(solution)/shard_map/reduce_scatter | solution.py:307
  90.0 6.4 %copy-start.6 = (bf16[1025,1024]{1,0:T(8,128)(2,1)S(1)}, bf16[1025,1024]{1,0:T(8,128)(2,1)}, u32[]{:S(2)}) copy-start(bf16[1025,1024]{1,0:T(8,128)(2,1)} %get-tuple-element.26) | copy-start | bytes 6297604
  90.0 6.4 %copy-start.8 = (bf16[1025,1024]{1,0:T(8,128)(2,1)S(1)}, bf16[1025,1024]{1,0:T(8,128)(2,1)}, u32[]{:S(2)}) copy-start(bf16[1025,1024]{1,0:T(8,128)(2,1)} %get-tuple-element.27) | copy-start | bytes 6297604
  90.0 6.4 %copy-start.9 = (f32[2050,256]{1,0:T(8,128)S(1)}, f32[2050,256]{1,0:T(8,128)}, u32[]{:S(2)}) copy-start(f32[2050,256]{1,0:T(8,128)} %pad_maximum_fusion.4) | copy-start | bytes 6297604
  90.0 6.4 %copy-start.13 = (f32[1025,256]{1,0:T(8,128)S(1)}, f32[1025,256]{1,0:T(8,128)}, u32[]{:S(2)}) copy-start(f32[1025,256]{1,0:T(8,128)} %get-tuple-element.20) | copy-start | bytes 3148804
  90.0 6.4 %copy-start.14 = (f32[1025,256]{1,0:T(8,128)S(1)}, f32[1025,256]{1,0:T(8,128)}, u32[]{:S(2)}) copy-start(f32[1025,256]{1,0:T(8,128)} %get-tuple-element.21) | copy-start | bytes 3148804
  96.4 2.9 %copy-start.11 = (bf16[1024,256]{1,0:T(8,128)(2,1)S(1)}, bf16[1024,256]{1,0:T(8,128)(2,1)}, u32[]{:S(2)}) copy-start(bf16[1024,256]{1,0:T(8,128)(2,1)} %copy-done.10) | copy-start | bytes 1572868
  99.2 2.1 %copy-start.1 = (bf16[8,128,5,256]{3,1,0,2:T(8,128)(2,1)S(1)}, bf16[8,128,5,256]{3,1,0,2:T(8,128)(2,1)}, u32[]{:S(2)}) copy-start(bf16[8,128,5,256]{3,1,0,2:T(8,128)(2,1)} %copy-done) | copy-start | bytes 7864324
  99.2 2.6 %copy-start.4 = (bf16[1024,3,256]{2,0,1:T(8,128)(2,1)S(1)}, bf16[1024,3,256]{2,0,1:T(8,128)(2,1)}, u32[]{:S(2)}) copy-start(bf16[1024,3,256]{2,0,1:T(8,128)(2,1)} %copy-done.3) | copy-start | bytes 4718596
  99.3 2.8 %copy-start.15 = (f32[1024,1,256]{2,0,1:T(8,128)S(1)}, f32[1024,1,256]{2,0,1:T(8,128)}, u32[]{:S(2)}) copy-start(f32[1024,1,256]{2,0,1:T(8,128)} %get-tuple-element.32) | copy-start | bytes 3145732
  127.6 24.5 %all-to-all-start.2 = ((bf16[8,128,3,256]{3,1,2,0:T(8,128)(2,1)}), bf16[8,128,3,256]{3,1,2,0:T(8,128)(2,1)S(1)}, u32[]{:S(2)}, u32[]{:S(2)}) async-start(bf16[8,128,3,256]{3,1,2,0:T(8,128)(2,1)} %copy.39), calls=%async_computation.2 | async-start | bytes 3145728 | tf_op jit(solution)/shard_map/all_to_all | solution.py:281
Sparse Core Ops, SparseCore 0:
  125.5 31.5 reduce-scatter.1

commit v4 on v2

--- a/solution.py
+++ b/solution.py
@@ -3,6 +3,7 @@
 import jax
 import jax.numpy as jnp
 from jax import lax
+from jax.experimental import pallas as pl
 from jax.sharding import PartitionSpec as P
 
 
@@ -240,6 +241,28 @@
     )
 
 
+def gather_tiles(features2d, cot2d, resp2d, seq_parts, narrow):
+    rows = features2d.shape[0]
+
+    def body(f0, f1, f2, c_ref, r_ref, out_ref):
+        out_ref[0, 0] = f0[...]
+        out_ref[0, 1] = f1[...]
+        out_ref[0, 2] = f2[...]
+        out_ref[0, 3] = c_ref[...]
+        out_ref[0, 4] = r_ref[...]
+
+    def group_spec(group):
+        return pl.BlockSpec((rows, narrow), lambda s: (0, group * seq_parts + s))
+
+    return pl.pallas_call(
+        body,
+        grid=(seq_parts,),
+        in_specs=[group_spec(0), group_spec(1), group_spec(2), group_spec(0), group_spec(0)],
+        out_specs=pl.BlockSpec((1, 5, rows, narrow), lambda s: (s, 0, 0, 0)),
+        out_shape=jax.ShapeDtypeStruct((seq_parts, 5, rows, narrow), features2d.dtype),
+    )(features2d, features2d, features2d, cot2d, resp2d)
+
+
 def local(features, short_filter, response, skip_gain, cotangent):
     seq_parts = lax.axis_size("seq")
     dp_parts = lax.axis_size("dp")
@@ -250,16 +273,30 @@
     narrow = chan_width // seq_parts
     offset = seq_index * narrow
     taps = short_filter.reshape(3, 3, chan_width)
-    joined_in = jnp.concatenate(
-        [
+    if narrow % 128 == 0 and tok_rows % 16 == 0:
+        arranged = gather_tiles(
             features.reshape(tok_rows, 3 * chan_width),
             cotangent.reshape(tok_rows, chan_width),
             response,
-        ],
-        axis=1,
-    )
-    arranged = joined_in.reshape(tok_rows, 5, seq_parts, narrow).transpose(2, 0, 1, 3)
-    moved_in = lax.all_to_all(arranged, "seq", 0, 0, tiled=True).reshape(length, 5, narrow)
+            seq_parts,
+            narrow,
+        )
+        moved_in = (
+            lax.all_to_all(arranged, "seq", 0, 0, tiled=True)
+            .transpose(0, 2, 1, 3)
+            .reshape(length, 5, narrow)
+        )
+    else:
+        joined_in = jnp.concatenate(
+            [
+                features.reshape(tok_rows, 3 * chan_width),
+                cotangent.reshape(tok_rows, chan_width),
+                response,
+            ],
+            axis=1,
+        )
+        arranged = joined_in.reshape(tok_rows, 5, seq_parts, narrow).transpose(2, 0, 1, 3)
+        moved_in = lax.all_to_all(arranged, "seq", 0, 0, tiled=True).reshape(length, 5, narrow)
     local_taps = lax.dynamic_slice_in_dim(taps, offset, narrow, 2)
     local_skip = lax.dynamic_slice_in_dim(skip_gain, offset, narrow, 0)
     if length <= 2048:

time: 154 us -> 145 us (0.942)
  local copies, waits for them, and re-layouts: 23.2 us -> 15.6 us
  other arithmetic: 37.6 us -> 30.6 us
  Pallas kernels: 0 us -> 5.9 us
    concatenate x1 -> x0, other arithmetic: 6.96 us -> none  [local(): jnp.concatenate([features.reshape(tok_rows, 3 * chan_width), cotangent.re...]
    pallas_call x0 -> x1, Pallas kernels: none -> 5.9 us  [gather_tiles(): pl.pallas_call(body, grid=(seq_parts,), in_specs=[group_spec(0), group_sp...]
    unnamed x19 -> x14, local copies, waits for them, and re-layouts: 12.1 us -> 7.08 us
    transpose x1, local copies, waits for them, and re-layouts: 2.59 us -> 0.28 us  [local(): moved_in = lax.all_to_all(arranged, 'seq', 0, 0, tiled=True).transpose(0,...]
  transfers between devices with their start and end apart: 2 -> 2, of which waited for: 1 -> 1; matrix products, arithmetic and copies ran while one was open for 21% -> 22% of each run, Pallas kernels for 0% -> 0%
where the time goes in v4:
time: 145 us; the launch traced here: 144 us
  blocking collectives  48.9 us (34%)
  other arithmetic  30.6 us (21%)
  local copies, waits for them, and re-layouts  15.6 us (11%)
  between operations  14.3 us (10%)
  matrix products  13.8 us (10%)
  waiting for transfers between devices  9.81 us (7%)
  Pallas kernels  5.9 us (4%)
  starting transfers between devices  5.34 us (4%)
    all_to_all x1, blocking collectives, local(): lax.all_to_all(joined_out, 'seq', 0, 0, tiled=True).transpose(1, 2, 0, 3)  29.8 us
    all_to_all x1, blocking collectives, local(): moved = lax.all_to_all(chunks, 'seq', 0, 0, tiled=True)  19.2 us
    another operation x1, other arithmetic  17.8 us
    dot_general x6, matrix products, bf16_dot(): lax.dot_general(left, right, (dims, ((), ())), preferred_element_type=jnp...  13.8 us
    all_to_all x1, waiting for transfers between devices, local(): lax.all_to_all(arranged, 'seq', 0, 0, tiled=True).transpose(0, 2, 1, 3)  9.8 us
    unnamed x14, local copies, waits for them, and re-layouts  7.08 us
    pallas_call x1, Pallas kernels, gather_tiles(): pl.pallas_call(body, grid=(seq_parts,), in_specs=[group_spec(0), group_sp...  5.9 us
    all_to_all x1, starting transfers between devices, local(): lax.all_to_all(arranged, 'seq', 0, 0, tiled=True).transpose(0, 2, 1, 3)  5.3 us
  transfers between devices with their start and end apart: 2, of which 1 were waited for; matrix products, arithmetic and copies ran while one was open for 22% of the time, Pallas kernels for 0%

profile of v4, /device:TPU:0, one launch (start us, length us, event | category | flops | bytes accessed | tf_op | source)
XLA Modules:
  0.0 144.3 jit_solution(3680381275516225711)
XLA Ops:
  7.2 5.9 %shard_map.92 = bf16[8,5,128,256]{3,2,1,0:T(8,128)(2,1)} custom-call(bf16[128,6144]{1,0:T(8,128)(2,1)} %bitcast.80, bf16[128,6144]{1,0:T(8,128)(2,1)} %bitcast.81, bf16[128,6144]{1,0:T(8,128)(2,1)} %bitcast.82, bf16[128,2048]{1,0:T(8,128)(2,1)} %bitcast.93, bf16[128,2048]{1,0:T(8,128)(2,1)} %r_ref.1), custom_call_target="tpu_custom_call" | custom-call | tf_op jit(solution)/shard_map/pallas_call | solution.py:257
  13.1 5.3 %all-to-all-start = ((bf16[8,5,128,256]{3,2,1,0:T(8,128)(2,1)}), bf16[8,5,128,256]{3,2,1,0:T(8,128)(2,1)S(1)}, u32[]{:S(2)}, u32[]{:S(2)}) async-start(bf16[8,5,128,256]{3,2,1,0:T(8,128)(2,1)} %shard_map.92), calls=%async_computation | async-start | bytes 5242880 | tf_op jit(solution)/shard_map/all_to_all | solution.py:285
  18.4 0.0 reduce-scatter.2.cloned.1.call-start
  18.4 0.1 reshape.87
  18.5 3.7 %add_select_fusion = s32[1025,1024]{1,0:T(8,128)} fusion(), kind=kLoop, calls=%fused_computation | loop fusion | flops 12595200 | bytes 4198400 | tf_op jit(solution)/shard_map/jit(remainder)/select_n | solution.py:130
  22.2 0.8 dynamic_slice.7
  23.0 0.1 pad.8.clone
  23.1 17.8 %cosine_convert_fusion = (bf16[1025,1024]{1,0:T(8,128)(2,1)}, bf16[1025,1024]{1,0:T(8,128)(2,1)}) fusion(s32[1025,1024]{1,0:T(8,128)} %add_select_fusion), kind=kLoop, calls=%fused_computation.5 | loop fusion | flops 5248000 | bytes 8396800 | tf_op jit(solution)/shard_map/convert.1
  40.8 9.8 %all-to-all-done = bf16[8,5,128,256]{3,2,1,0:T(8,128)(2,1)S(1)} async-done(((bf16[8,5,128,256]{3,2,1,0:T(8,128)(2,1)}), bf16[8,5,128,256]{3,2,1,0:T(8,128)(2,1)S(1)}, u32[]{:S(2)}, u32[]{:S(2)}) %all-to-all-start) | async-done | bytes 2621472 | tf_op jit(solution)/shard_map/all_to_all | solution.py:285
  50.6 0.3 copy.32
  50.9 0.1 slice.129
  51.1 1.0 fusion.7
  52.1 0.3 fusion.22
  52.5 1.2 copy-done
  53.7 0.6 copy-done.1
  54.3 1.4 fusion.41
  55.8 2.5 %fusion.25 = f32[2050,512]{1,0:T(8,128)S(1)} fusion(bf16[1024,256]{1,0:T(8,128)(2,1)S(1)} %slice_bitcast_fusion.4, bf16[1024,256]{1,0:T(8,128)(2,1)S(1)} %get-tuple-element.14, bf16[1025,1024]{1,0:T(8,128)(2,1)S(1)} %copy-done.1, bf16[1025,1024]{1,0:T(8,128)(2,1)S(1)} %copy-done), kind=kOutput, calls=%fused_computation.64 | convolution fusion | flops 2160074752 | bytes 9445376 | tf_op jit(solution)/shard_map/dot_general | solution.py:138
  58.2 0.3 multiply_subtract_fusion.2
  58.6 0.7 multiply_add_fusion.1
  59.2 2.8 %fusion.30 = f32[1024,512]{1,0:T(8,128)S(1)} fusion(f32[1025,256]{1,0:T(8,128)S(1)} %get-tuple-element.18, f32[1025,256]{1,0:T(8,128)S(1)} %get-tuple-element.17, f32[1025,256]{1,0:T(8,128)S(1)} %get-tuple-element.19, f32[1025,256]{1,0:T(8,128)S(1)} %get-tuple-element.16, f32[2050]{0:T(1024)S(1)} %fusion.35, bf16[1025,1024]{1,0:T(8,128)(2,1)S(1)} %copy-done.1, ...), kind=kOutput, calls=%fused_computation.74 | convolution fusion | flops 2163225600 | bytes 10502152 | tf_op jit(solution)/shard_map/dot_general | solution.py:138
  62.0 2.9 %fusion.15 = f32[1024,512]{1,0:T(8,128)S(1)} fusion(f32[1024,512]{1,0:T(8,128)S(1)} %fusion.30, f32[1025,256]{1,0:T(8,128)S(1)} %get-tuple-element.18, f32[1025,256]{1,0:T(8,128)S(1)} %get-tuple-element.17, f32[1025,256]{1,0:T(8,128)S(1)} %get-tuple-element.19, f32[1025,256]{1,0:T(8,128)S(1)} %get-tuple-element.16, f32[2050]{0:T(1024)S(1)} %fusion.35, ...), kind=kOutput, calls=%fused_computation.36 | convolution fusion | flops 2166898688 | bytes 12599304 | tf_op jit(solution)/shard_map/dot_general | solution.py:138
  64.9 2.2 %fusion.17 = f32[1024,256]{1,0:T(8,128)S(1)} fusion(f32[1025,256]{1,0:T(8,128)S(1)} %get-tuple-element.25, f32[1025,256]{1,0:T(8,128)S(1)} %get-tuple-element.24, f32[2050]{0:T(1024)S(1)} %fusion.35, bf16[1025,1024]{1,0:T(8,128)(2,1)S(1)} %copy-done.1, bf16[1025,1024]{1,0:T(8,128)(2,1)S(1)} %copy-done), kind=kOutput, calls=%fused_computation.48 | convolution fusion | flops 1084761600 | bytes 7354376 | tf_op jit(solution)/shard_map/dot_general | solution.py:138
  67.1 2.1 %fusion.16 = f32[1024,256]{1,0:T(8,128)S(1)} fusion(f32[1024,256]{1,0:T(8,128)S(1)} %fusion.17, f32[1025,256]{1,0:T(8,128)S(1)} %get-tuple-element.25, f32[1025,256]{1,0:T(8,128)S(1)} %get-tuple-element.24, f32[2050]{0:T(1024)S(1)} %fusion.35, bf16[1024,256]{1,0:T(8,128)(2,1)S(1)} %get-tuple-element.14, f32[256]{0:T(256)S(1)} %dynamic_slice.7, ...), kind=kOutput, calls=%fused_computation.46 | convolution fusion | flops 1087384576 | bytes 8928264 | tf_op jit(solution)/shard_map/dot_general | solution.py:138
  69.2 0.2 fusion.23
  69.4 1.6 %multiply_bitcast_fusion.1 = (f32[1024,1,256]{2,0,1:T(8,128)S(1)}, f32[1024,1,256]{2,0,1:T(8,128)S(1)}, bf16[1024,256]{1,0:T(8,128)(2,1)}, f32[1024,256]{1,0:T(8,128)}) fusion(f32[1024,3,256]{2,0,1:T(8,128)S(1)} %fusion.7, bf16[1024,256]{1,0:T(8,128)(2,1)S(1)} %get-tuple-element.15, f32[1024,512]{1,0:T(8,128)S(1)} %fusion.15, f32[256]{0:T(256)S(1)} %dynamic_slice.7, ...), kind=kLoop, calls=%fused_computation.69 | loop fusion | flops 1835008 | bytes 10486784 | tf_op jit(solution)/shard_map/stack | solution.py:192
  71.0 1.3 fusion.9
  72.3 0.1 maximum_maximum_fusion
  72.4 1.3 pad_maximum_fusion.6
  73.7 19.2 %all_to_all.15 = f32[8,144,256]{2,1,0:T(8,128)S(1)} all-to-all(f32[8,144,256]{2,1,0:T(8,128)S(1)} %pad_maximum_fusion.6), channel_id=1, replica_groups=mesh['dp'=4,'seq'=8] {'seq'}, dimensions={0} | all-to-all | bytes 2359296 | tf_op jit(solution)/shard_map/all_to_all | solution.py:331
  92.9 0.1 copy.36
  93.0 0.1 slice.145
  93.1 1.2 pad_maximum_fusion.5
  94.3 0.0 reduce-scatter.2.cloned.1.call-update
  94.3 0.0 copy-start.2
  94.3 1.0 add_convert_fusion
  95.3 0.0 copy-done.2
  95.3 0.2 pad_maximum_fusion.4
  95.6 29.8 %all_to_all.16 = bf16[8,128,4,256]{3,1,2,0:T(8,128)(2,1)} all-to-all(bf16[8,128,4,256]{3,1,2,0:T(8,128)(2,1)S(1)} %pad_maximum_fusion.4), channel_id=1, replica_groups=mesh['dp'=4,'seq'=8] {'seq'}, dimensions={0} | all-to-all | bytes 4194304 | tf_op jit(solution)/shard_map/all_to_all | solution.py:316
  125.3 3.0 %copy.35 = bf16[8,128,4,256]{1,3,0,2:T(8,128)(2,1)S(1)} copy(bf16[8,128,4,256]{3,1,2,0:T(8,128)(2,1)} %all_to_all.16) | data formatting | bytes 4194304 | tf_op jit(solution)/shard_map/all_to_all | solution.py:316
  128.4 1.3 slice.143
  129.7 1.0 copy.41
  130.7 2.6 %copy.42 = bf16[1,128,6144]{2,1,0:T(8,128)(2,1)} copy(bf16[1,128,6144]{1,2,0:T(8,128)(2,1)} %bitcast.86) | data formatting | bytes 3145728
  133.2 0.9 slice.147
  134.2 0.7 reshape.98
  135.0 0.6 copy.45
  135.6 1.0 slice.150
  136.5 0.1 copy.44
  136.7 0.8 copy.43
  (20 shorter events, 0.2 us)
Async XLA Ops:
  13.1 5.4 %copy-start.3 = (f32[3,6144]{1,0:T(4,128)S(1)}, f32[3,6144]{1,0:T(4,128)}, u32[]{:S(2)}) copy-start(f32[3,6144]{1,0:T(4,128)} %param.6) | copy-start | bytes 221188
  13.1 37.6 %all-to-all-start = ((bf16[8,5,128,256]{3,2,1,0:T(8,128)(2,1)}), bf16[8,5,128,256]{3,2,1,0:T(8,128)(2,1)S(1)}, u32[]{:S(2)}, u32[]{:S(2)}) async-start(bf16[8,5,128,256]{3,2,1,0:T(8,128)(2,1)} %shard_map.92), calls=%async_computation | async-start | bytes 5242880 | tf_op jit(solution)/shard_map/all_to_all | solution.py:285
  18.4 114.9 %reduce-scatter.2.cloned.1.call-start = ((), (), s32[]{:S(2)}) async-start(), calls=%async_computation.4 | async-start | bytes 1720320 | tf_op jit(solution)/shard_map/reduce_scatter | solution.py:342
  52.1 1.6 %copy-start = (bf16[1025,1024]{1,0:T(8,128)(2,1)S(1)}, bf16[1025,1024]{1,0:T(8,128)(2,1)}, u32[]{:S(2)}) copy-start(bf16[1025,1024]{1,0:T(8,128)(2,1)} %get-tuple-element.22) | copy-start | bytes 6297604
  52.1 2.2 %copy-start.1 = (bf16[1025,1024]{1,0:T(8,128)(2,1)S(1)}, bf16[1025,1024]{1,0:T(8,128)(2,1)}, u32[]{:S(2)}) copy-start(bf16[1025,1024]{1,0:T(8,128)(2,1)} %get-tuple-element.23) | copy-start | bytes 6297604
  94.3 1.0 copy-start.2
Sparse Core Ops, SparseCore 0:
  94.4 31.5 reduce-scatter.1

commit v5 on v4

--- a/solution.py
+++ b/solution.py
@@ -263,6 +263,38 @@
     )(features2d, features2d, features2d, cot2d, resp2d)
 
 
+def scatter_tiles(moved, seq_parts, narrow):
+    rows = moved.shape[2]
+
+    def body(in_ref, gated_ref, feats_ref):
+        group = pl.program_id(0)
+
+        @pl.when(group == 0)
+        def _():
+            for source in range(seq_parts):
+                gated_ref[:, source * narrow : (source + 1) * narrow] = in_ref[source, 0]
+
+        @pl.when(group > 0)
+        def _():
+            for source in range(seq_parts):
+                feats_ref[:, source * narrow : (source + 1) * narrow] = in_ref[source, 0]
+
+    width = seq_parts * narrow
+    return pl.pallas_call(
+        body,
+        grid=(4,),
+        in_specs=[pl.BlockSpec((seq_parts, 1, rows, narrow), lambda g: (0, g, 0, 0))],
+        out_specs=[
+            pl.BlockSpec((rows, width), lambda g: (0, 0)),
+            pl.BlockSpec((rows, width), lambda g: (0, jnp.maximum(g - 1, 0))),
+        ],
+        out_shape=[
+            jax.ShapeDtypeStruct((rows, width), moved.dtype),
+            jax.ShapeDtypeStruct((rows, 3 * width), moved.dtype),
+        ],
+    )(moved)
+
+
 def local(features, short_filter, response, skip_gain, cotangent):
     seq_parts = lax.axis_size("seq")
     dp_parts = lax.axis_size("dp")
@@ -309,13 +341,24 @@
         )
         gated = gated.reshape(length, narrow)
         grad_feats = grad_feats.reshape(length, 3, narrow)
-    joined_out = jnp.concatenate(
-        [gated.reshape(seq_parts, tok_rows, 1, narrow), grad_feats.reshape(seq_parts, tok_rows, 3, narrow)],
-        axis=2,
-    )
-    moved_out = lax.all_to_all(joined_out, "seq", 0, 0, tiled=True).transpose(1, 2, 0, 3)
-    gated = moved_out[:, 0]
-    grad_feats = moved_out[:, 1:]
+    if narrow % 128 == 0 and tok_rows % 16 == 0:
+        joined_out = jnp.concatenate(
+            [
+                gated.reshape(seq_parts, 1, tok_rows, narrow),
+                grad_feats.reshape(seq_parts, tok_rows, 3, narrow).transpose(0, 2, 1, 3),
+            ],
+            axis=1,
+        )
+        moved_out = lax.all_to_all(joined_out, "seq", 0, 0, tiled=True)
+        gated, grad_feats = scatter_tiles(moved_out, seq_parts, narrow)
+    else:
+        joined_out = jnp.concatenate(
+            [gated.reshape(seq_parts, tok_rows, 1, narrow), grad_feats.reshape(seq_parts, tok_rows, 3, narrow)],
+            axis=2,
+        )
+        moved_out = lax.all_to_all(joined_out, "seq", 0, 0, tiled=True).transpose(1, 2, 0, 3)
+        gated = moved_out[:, 0]
+        grad_feats = moved_out[:, 1:]
     extra = 16
     small = jnp.concatenate(
         [grad_taps.reshape(9, narrow), grad_skip[None], jnp.zeros((extra - 10, narrow), jnp.float32)],

time: 145 us -> 142 us (0.979)
  local copies, waits for them, and re-layouts: 15.6 us -> 8.66 us
  Pallas kernels: 5.9 us -> 9.47 us
    pallas_call x0 -> x1, Pallas kernels: none -> 3.56 us  [scatter_tiles(): pl.pallas_call(body, grid=(4,), in_specs=[pl.BlockSpec((seq_parts, 1, row...]
    all_to_all x1 -> x0, local copies, waits for them, and re-layouts: 3.04 us -> none  [local(): lax.all_to_all(joined_out, 'seq', 0, 0, tiled=True).transpose(1, 2, 0, 3)]
    unnamed x14 -> x12, local copies, waits for them, and re-layouts: 7.08 us -> 4.33 us
  transfers between devices with their start and end apart: 2 -> 2, of which waited for: 1 -> 1; matrix products, arithmetic and copies ran while one was open for 22% -> 17% of each run, Pallas kernels for 0% -> 3%
where the time goes in v5:
time: 142 us; the launch traced here: 141 us
  blocking collectives  48.9 us (34%)
  other arithmetic  30.7 us (22%)
  between operations  14.3 us (10%)
  matrix products  13.8 us (10%)
  waiting for transfers between devices  9.82 us (7%)
  Pallas kernels  9.47 us (7%)
  local copies, waits for them, and re-layouts  8.66 us (6%)
  starting transfers between devices  5.34 us (4%)
    all_to_all x1, blocking collectives, local(): moved_out = lax.all_to_all(joined_out, 'seq', 0, 0, tiled=True)  29.7 us
    all_to_all x1, blocking collectives, local(): moved = lax.all_to_all(chunks, 'seq', 0, 0, tiled=True)  19.2 us
    another operation x1, other arithmetic  17.8 us
    dot_general x6, matrix products, bf16_dot(): lax.dot_general(left, right, (dims, ((), ())), preferred_element_type=jnp...  13.8 us
    all_to_all x1, waiting for transfers between devices, local(): lax.all_to_all(arranged, 'seq', 0, 0, tiled=True).transpose(0, 2, 1, 3)  9.8 us
    pallas_call x1, Pallas kernels, gather_tiles(): pl.pallas_call(body, grid=(seq_parts,), in_specs=[group_spec(0), group_sp...  5.92 us
    all_to_all x1, starting transfers between devices, local(): lax.all_to_all(arranged, 'seq', 0, 0, tiled=True).transpose(0, 2, 1, 3)  5.3 us
    unnamed x12, local copies, waits for them, and re-layouts  4.33 us
  transfers between devices with their start and end apart: 2, of which 1 were waited for; matrix products, arithmetic and copies ran while one was open for 17% of the time, Pallas kernels for 3%

profile of v5, /device:TPU:0, one launch (start us, length us, event | category | flops | bytes accessed | tf_op | source)
XLA Modules:
  0.0 141.0 jit_solution(16155781097704090528)
XLA Ops:
  7.2 5.9 %shard_map.92 = bf16[8,5,128,256]{3,2,1,0:T(8,128)(2,1)} custom-call(bf16[128,6144]{1,0:T(8,128)(2,1)} %bitcast.80, bf16[128,6144]{1,0:T(8,128)(2,1)} %bitcast.81, bf16[128,6144]{1,0:T(8,128)(2,1)} %bitcast.82, bf16[128,2048]{1,0:T(8,128)(2,1)} %bitcast.90, bf16[128,2048]{1,0:T(8,128)(2,1)} %r_ref.1), custom_call_target="tpu_custom_call" | custom-call | tf_op jit(solution)/shard_map/pallas_call | solution.py:257
  13.1 5.3 %all-to-all-start = ((bf16[8,5,128,256]{3,2,1,0:T(8,128)(2,1)}), bf16[8,5,128,256]{3,2,1,0:T(8,128)(2,1)S(1)}, u32[]{:S(2)}, u32[]{:S(2)}) async-start(bf16[8,5,128,256]{3,2,1,0:T(8,128)(2,1)} %shard_map.92), calls=%async_computation | async-start | bytes 5242880 | tf_op jit(solution)/shard_map/all_to_all | solution.py:317
  18.4 0.0 reduce-scatter.2.cloned.1.call-start
  18.4 0.0 copy-done.3
  18.4 0.1 reshape.90
  18.5 3.7 %add_select_fusion = s32[1025,1024]{1,0:T(8,128)} fusion(), kind=kLoop, calls=%fused_computation | loop fusion | flops 12595200 | bytes 4198400 | tf_op jit(solution)/shard_map/jit(remainder)/select_n | solution.py:130
  22.2 0.8 dynamic_slice.7
  23.0 0.1 pad.8.clone
  23.1 17.8 %cosine_convert_fusion = (bf16[1025,1024]{1,0:T(8,128)(2,1)}, bf16[1025,1024]{1,0:T(8,128)(2,1)}) fusion(s32[1025,1024]{1,0:T(8,128)} %add_select_fusion), kind=kLoop, calls=%fused_computation.5 | loop fusion | flops 5248000 | bytes 8396800 | tf_op jit(solution)/shard_map/convert.1
  40.8 9.8 %all-to-all-done = bf16[8,5,128,256]{3,2,1,0:T(8,128)(2,1)S(1)} async-done(((bf16[8,5,128,256]{3,2,1,0:T(8,128)(2,1)}), bf16[8,5,128,256]{3,2,1,0:T(8,128)(2,1)S(1)}, u32[]{:S(2)}, u32[]{:S(2)}) %all-to-all-start) | async-done | bytes 2621472 | tf_op jit(solution)/shard_map/all_to_all | solution.py:317
  50.7 0.3 copy.27
  50.9 0.1 slice.121
  51.1 1.0 fusion.7
  52.1 0.0 copy-start
  52.1 0.3 fusion.22
  52.5 1.2 copy-done
  53.7 0.6 copy-done.1
  54.4 1.4 fusion.41
  55.8 2.4 %fusion.25 = f32[2050,512]{1,0:T(8,128)S(1)} fusion(bf16[1024,256]{1,0:T(8,128)(2,1)S(1)} %slice_bitcast_fusion.4, bf16[1024,256]{1,0:T(8,128)(2,1)S(1)} %get-tuple-element.18, bf16[1025,1024]{1,0:T(8,128)(2,1)S(1)} %copy-done.1, bf16[1025,1024]{1,0:T(8,128)(2,1)S(1)} %copy-done), kind=kOutput, calls=%fused_computation.65 | convolution fusion | flops 2160074752 | bytes 9445376 | tf_op jit(solution)/shard_map/dot_general | solution.py:138
  58.2 0.3 multiply_subtract_fusion.2
  58.6 0.8 multiply_add_fusion.1
  59.3 2.8 %fusion.30 = f32[1024,512]{1,0:T(8,128)S(1)} fusion(f32[1025,256]{1,0:T(8,128)S(1)} %get-tuple-element.22, f32[1025,256]{1,0:T(8,128)S(1)} %get-tuple-element.21, f32[1025,256]{1,0:T(8,128)S(1)} %get-tuple-element.23, f32[1025,256]{1,0:T(8,128)S(1)} %get-tuple-element.20, f32[2050]{0:T(1024)S(1)} %fusion.35, bf16[1025,1024]{1,0:T(8,128)(2,1)S(1)} %copy-done.1, ...), kind=kOutput, calls=%fused_computation.75 | convolution fusion | flops 2163225600 | bytes 10502152 | tf_op jit(solution)/shard_map/dot_general | solution.py:138
  62.1 2.8 %fusion.15 = f32[1024,512]{1,0:T(8,128)S(1)} fusion(f32[1024,512]{1,0:T(8,128)S(1)} %fusion.30, f32[1025,256]{1,0:T(8,128)S(1)} %get-tuple-element.22, f32[1025,256]{1,0:T(8,128)S(1)} %get-tuple-element.21, f32[1025,256]{1,0:T(8,128)S(1)} %get-tuple-element.23, f32[1025,256]{1,0:T(8,128)S(1)} %get-tuple-element.20, f32[2050]{0:T(1024)S(1)} %fusion.35, ...), kind=kOutput, calls=%fused_computation.37 | convolution fusion | flops 2166898688 | bytes 12599304 | tf_op jit(solution)/shard_map/dot_general | solution.py:138
  65.0 2.2 %fusion.17 = f32[1024,256]{1,0:T(8,128)S(1)} fusion(f32[1025,256]{1,0:T(8,128)S(1)} %get-tuple-element.29, f32[1025,256]{1,0:T(8,128)S(1)} %get-tuple-element.28, f32[2050]{0:T(1024)S(1)} %fusion.35, bf16[1025,1024]{1,0:T(8,128)(2,1)S(1)} %copy-done.1, bf16[1025,1024]{1,0:T(8,128)(2,1)S(1)} %copy-done), kind=kOutput, calls=%fused_computation.49 | convolution fusion | flops 1084761600 | bytes 7354376 | tf_op jit(solution)/shard_map/dot_general | solution.py:138
  67.2 2.1 %fusion.16 = f32[1024,256]{1,0:T(8,128)S(1)} fusion(f32[1024,256]{1,0:T(8,128)S(1)} %fusion.17, f32[1025,256]{1,0:T(8,128)S(1)} %get-tuple-element.29, f32[1025,256]{1,0:T(8,128)S(1)} %get-tuple-element.28, f32[2050]{0:T(1024)S(1)} %fusion.35, bf16[1024,256]{1,0:T(8,128)(2,1)S(1)} %get-tuple-element.18, f32[256]{0:T(256)S(1)} %dynamic_slice.7, ...), kind=kOutput, calls=%fused_computation.47 | convolution fusion | flops 1087384576 | bytes 8928264 | tf_op jit(solution)/shard_map/dot_general | solution.py:138
  69.3 0.2 fusion.23
  69.5 1.6 %multiply_bitcast_fusion.1 = (f32[1024,1,256]{2,0,1:T(8,128)S(1)}, f32[1024,1,256]{2,0,1:T(8,128)S(1)}, bf16[1024,256]{1,0:T(8,128)(2,1)}, f32[1024,256]{1,0:T(8,128)}) fusion(f32[1024,3,256]{2,0,1:T(8,128)S(1)} %fusion.7, bf16[1024,256]{1,0:T(8,128)(2,1)S(1)} %get-tuple-element.19, f32[1024,512]{1,0:T(8,128)S(1)} %fusion.15, f32[256]{0:T(256)S(1)} %dynamic_slice.7, ...), kind=kLoop, calls=%fused_computation.70 | loop fusion | flops 1835008 | bytes 10486784 | tf_op jit(solution)/shard_map/stack | solution.py:192
  71.1 1.3 fusion.9
  72.4 0.1 maximum_maximum_fusion
  72.5 1.3 pad_maximum_fusion.6
  73.8 19.2 %all_to_all.15 = f32[8,144,256]{2,1,0:T(8,128)S(1)} all-to-all(f32[8,144,256]{2,1,0:T(8,128)S(1)} %pad_maximum_fusion.6), channel_id=1, replica_groups=mesh['dp'=4,'seq'=8] {'seq'}, dimensions={0} | all-to-all | bytes 2359296 | tf_op jit(solution)/shard_map/all_to_all | solution.py:374
  93.0 0.1 copy.29
  93.1 0.1 slice.135
  93.2 1.2 pad_maximum_fusion.5
  94.4 0.0 reduce-scatter.2.cloned.1.call-update
  94.4 1.0 add_convert_fusion
  95.4 0.0 copy-start.2
  95.4 0.1 copy.38
  95.5 0.9 copy-done.2
  96.4 0.2 pad_maximum_fusion.4
  96.6 29.7 %all_to_all.16.in_ref = bf16[8,4,128,256]{3,2,1,0:T(8,128)(2,1)} all-to-all(bf16[8,4,128,256]{3,2,1,0:T(8,128)(2,1)S(1)} %pad_maximum_fusion.4), channel_id=1, replica_groups=mesh['dp'=4,'seq'=8] {'seq'}, dimensions={0} | all-to-all | bytes 4194304 | tf_op jit(solution)/shard_map/all_to_all | solution.py:352
  126.4 3.6 %shard_map.93 = (bf16[128,2048]{1,0:T(8,128)(2,1)}, bf16[128,6144]{1,0:T(8,128)(2,1)}) custom-call(bf16[8,4,128,256]{3,2,1,0:T(8,128)(2,1)} %all_to_all.16.in_ref), custom_call_target="tpu_custom_call" | custom-call | tf_op jit(solution)/shard_map/pallas_call | solution.py:283
  129.9 0.9 slice.137
  130.9 0.7 reshape.102
  131.6 0.6 copy.36
  132.2 1.0 slice.140
  133.2 0.1 copy.35
  133.3 0.8 copy.34
  (17 shorter events, 0.2 us)
Async XLA Ops:
  13.1 5.4 %copy-start.3 = (f32[3,6144]{1,0:T(4,128)S(1)}, f32[3,6144]{1,0:T(4,128)}, u32[]{:S(2)}) copy-start(f32[3,6144]{1,0:T(4,128)} %param.6) | copy-start | bytes 221188
  13.1 37.6 %all-to-all-start = ((bf16[8,5,128,256]{3,2,1,0:T(8,128)(2,1)}), bf16[8,5,128,256]{3,2,1,0:T(8,128)(2,1)S(1)}, u32[]{:S(2)}, u32[]{:S(2)}) async-start(bf16[8,5,128,256]{3,2,1,0:T(8,128)(2,1)} %shard_map.92), calls=%async_computation | async-start | bytes 5242880 | tf_op jit(solution)/shard_map/all_to_all | solution.py:317
  18.4 111.5 %reduce-scatter.2.cloned.1.call-start = ((), (), s32[]{:S(2)}) async-start(), calls=%async_computation.4 | async-start | bytes 1720320 | tf_op jit(solution)/shard_map/reduce_scatter | solution.py:385
  52.1 1.6 %copy-start = (bf16[1025,1024]{1,0:T(8,128)(2,1)S(1)}, bf16[1025,1024]{1,0:T(8,128)(2,1)}, u32[]{:S(2)}) copy-start(bf16[1025,1024]{1,0:T(8,128)(2,1)} %get-tuple-element.26) | copy-start | bytes 6297604
  52.1 2.2 %copy-start.1 = (bf16[1025,1024]{1,0:T(8,128)(2,1)S(1)}, bf16[1025,1024]{1,0:T(8,128)(2,1)}, u32[]{:S(2)}) copy-start(bf16[1025,1024]{1,0:T(8,128)(2,1)} %get-tuple-element.27) | copy-start | bytes 6297604
  95.4 1.0 copy-start.2
Sparse Core Ops, SparseCore 0:
  94.5 31.6 reduce-scatter.1

commit v6 on v5

--- a/solution.py
+++ b/solution.py
@@ -243,24 +243,38 @@
 
 def gather_tiles(features2d, cot2d, resp2d, seq_parts, narrow):
     rows = features2d.shape[0]
-
-    def body(f0, f1, f2, c_ref, r_ref, out_ref):
-        out_ref[0, 0] = f0[...]
-        out_ref[0, 1] = f1[...]
-        out_ref[0, 2] = f2[...]
-        out_ref[0, 3] = c_ref[...]
-        out_ref[0, 4] = r_ref[...]
-
-    def group_spec(group):
-        return pl.BlockSpec((rows, narrow), lambda s: (0, group * seq_parts + s))
+    width = seq_parts * narrow
+
+    def body(f_ref, c_ref, r_ref, out_ref):
+        group = pl.program_id(0)
+
+        def spread(src_ref):
+            for dest in range(seq_parts):
+                out_ref[dest, 0] = src_ref[:, dest * narrow : (dest + 1) * narrow]
+
+        @pl.when(group < 3)
+        def _():
+            spread(f_ref)
+
+        @pl.when(group == 3)
+        def _():
+            spread(c_ref)
+
+        @pl.when(group == 4)
+        def _():
+            spread(r_ref)
 
     return pl.pallas_call(
         body,
-        grid=(seq_parts,),
-        in_specs=[group_spec(0), group_spec(1), group_spec(2), group_spec(0), group_spec(0)],
-        out_specs=pl.BlockSpec((1, 5, rows, narrow), lambda s: (s, 0, 0, 0)),
+        grid=(5,),
+        in_specs=[
+            pl.BlockSpec((rows, width), lambda g: (0, jnp.minimum(g, 2))),
+            pl.BlockSpec((rows, width), lambda g: (0, 0)),
+            pl.BlockSpec((rows, width), lambda g: (0, 0)),
+        ],
+        out_specs=pl.BlockSpec((seq_parts, 1, rows, narrow), lambda g: (0, g, 0, 0)),
         out_shape=jax.ShapeDtypeStruct((seq_parts, 5, rows, narrow), features2d.dtype),
-    )(features2d, features2d, features2d, cot2d, resp2d)
+    )(features2d, cot2d, resp2d)
 
 
 def scatter_tiles(moved, seq_parts, narrow):

time: 142 us -> 140 us (0.986)
  no operation moved by 1% of the time
where the time goes in v6:
time: 140 us
  blocking collectives  48.9 us (35%)
  other arithmetic  30.7 us (22%)
  between operations  14.3 us (10%)
  matrix products  13.8 us (10%)
  waiting for transfers between devices  9.82 us (7%)
  local copies, waits for them, and re-layouts  8.66 us (6%)
  Pallas kernels  8.21 us (6%)
  starting transfers between devices  5.34 us (4%)
    all_to_all x1, blocking collectives, local(): moved_out = lax.all_to_all(joined_out, 'seq', 0, 0, tiled=True)  29.7 us
    all_to_all x1, blocking collectives, local(): moved = lax.all_to_all(chunks, 'seq', 0, 0, tiled=True)  19.2 us
    another operation x1, other arithmetic  17.8 us
    dot_general x6, matrix products, bf16_dot(): lax.dot_general(left, right, (dims, ((), ())), preferred_element_type=jnp...  13.8 us
    all_to_all x1, waiting for transfers between devices, local(): lax.all_to_all(arranged, 'seq', 0, 0, tiled=True).transpose(0, 2, 1, 3)  9.8 us
    all_to_all x1, starting transfers between devices, local(): lax.all_to_all(arranged, 'seq', 0, 0, tiled=True).transpose(0, 2, 1, 3)  5.3 us
    pallas_call x1, Pallas kernels, gather_tiles(): pl.pallas_call(body, grid=(5,), in_specs=[pl.BlockSpec((rows, width), lam...  4.65 us
    unnamed x12, local copies, waits for them, and re-layouts  4.33 us
  transfers between devices with their start and end apart: 2, of which 1 were waited for; matrix products, arithmetic and copies ran while one was open for 17% of the time, Pallas kernels for 3%

profile of v6, /device:TPU:0, one launch (start us, length us, event | category | flops | bytes accessed | tf_op | source)
XLA Modules:
  0.0 139.8 jit_solution(14582591963111678118)
XLA Ops:
  7.2 4.7 %shard_map.92 = bf16[8,5,128,256]{3,2,1,0:T(8,128)(2,1)} custom-call(bf16[128,6144]{1,0:T(8,128)(2,1)} %bitcast.85, bf16[128,2048]{1,0:T(8,128)(2,1)} %bitcast.88, bf16[128,2048]{1,0:T(8,128)(2,1)} %r_ref.1), custom_call_target="tpu_custom_call" | custom-call | tf_op jit(solution)/shard_map/pallas_call | solution.py:267
  11.8 5.3 %all-to-all-start = ((bf16[8,5,128,256]{3,2,1,0:T(8,128)(2,1)}), bf16[8,5,128,256]{3,2,1,0:T(8,128)(2,1)S(1)}, u32[]{:S(2)}, u32[]{:S(2)}) async-start(bf16[8,5,128,256]{3,2,1,0:T(8,128)(2,1)} %shard_map.92), calls=%async_computation | async-start | bytes 5242880 | tf_op jit(solution)/shard_map/all_to_all | solution.py:331
  17.1 0.0 reduce-scatter.2.cloned.1.call-start
  17.2 0.0 copy-done.3
  17.2 0.1 reshape.90
  17.3 3.7 %add_select_fusion = s32[1025,1024]{1,0:T(8,128)} fusion(), kind=kLoop, calls=%fused_computation | loop fusion | flops 12595200 | bytes 4198400 | tf_op jit(solution)/shard_map/jit(remainder)/select_n | solution.py:130
  21.0 0.8 dynamic_slice.7
  21.7 0.1 pad.8.clone
  21.8 17.8 %cosine_convert_fusion = (bf16[1025,1024]{1,0:T(8,128)(2,1)}, bf16[1025,1024]{1,0:T(8,128)(2,1)}) fusion(s32[1025,1024]{1,0:T(8,128)} %add_select_fusion), kind=kLoop, calls=%fused_computation.5 | loop fusion | flops 5248000 | bytes 8396800 | tf_op jit(solution)/shard_map/convert.1
  39.6 9.8 %all-to-all-done = bf16[8,5,128,256]{3,2,1,0:T(8,128)(2,1)S(1)} async-done(((bf16[8,5,128,256]{3,2,1,0:T(8,128)(2,1)}), bf16[8,5,128,256]{3,2,1,0:T(8,128)(2,1)S(1)}, u32[]{:S(2)}, u32[]{:S(2)}) %all-to-all-start) | async-done | bytes 2621472 | tf_op jit(solution)/shard_map/all_to_all | solution.py:331
  49.4 0.3 copy.27
  49.7 0.1 slice.121
  49.8 1.0 fusion.7
  50.9 0.0 copy-start
  50.9 0.3 fusion.22
  51.2 1.2 copy-done
  52.5 0.6 copy-done.1
  53.1 1.4 %fusion.41 = f32[2050,256]{1,0:T(8,128)S(1)} fusion(bf16[1024,256]{1,0:T(8,128)(2,1)S(1)} %get-tuple-element.19, bf16[1025,1024]{1,0:T(8,128)(2,1)S(1)} %copy-done.1, bf16[1025,1024]{1,0:T(8,128)(2,1)S(1)} %copy-done), kind=kOutput, calls=%fused_computation.95 | convolution fusion | flops 1083187200 | bytes 6821888 | tf_op jit(solution)/shard_map/dot_general | solution.py:138
  54.5 2.4 %fusion.25 = f32[2050,512]{1,0:T(8,128)S(1)} fusion(bf16[1024,256]{1,0:T(8,128)(2,1)S(1)} %slice_bitcast_fusion.4, bf16[1024,256]{1,0:T(8,128)(2,1)S(1)} %get-tuple-element.18, bf16[1025,1024]{1,0:T(8,128)(2,1)S(1)} %copy-done.1, bf16[1025,1024]{1,0:T(8,128)(2,1)S(1)} %copy-done), kind=kOutput, calls=%fused_computation.65 | convolution fusion | flops 2160074752 | bytes 9445376 | tf_op jit(solution)/shard_map/dot_general | solution.py:138
  56.9 0.3 multiply_subtract_fusion.2
  57.3 0.8 multiply_add_fusion.1
  58.1 2.8 %fusion.30 = f32[1024,512]{1,0:T(8,128)S(1)} fusion(f32[1025,256]{1,0:T(8,128)S(1)} %get-tuple-element.22, f32[1025,256]{1,0:T(8,128)S(1)} %get-tuple-element.21, f32[1025,256]{1,0:T(8,128)S(1)} %get-tuple-element.23, f32[1025,256]{1,0:T(8,128)S(1)} %get-tuple-element.20, f32[2050]{0:T(1024)S(1)} %fusion.35, bf16[1025,1024]{1,0:T(8,128)(2,1)S(1)} %copy-done.1, ...), kind=kOutput, calls=%fused_computation.75 | convolution fusion | flops 2163225600 | bytes 10502152 | tf_op jit(solution)/shard_map/dot_general | solution.py:138
  60.9 2.8 %fusion.15 = f32[1024,512]{1,0:T(8,128)S(1)} fusion(f32[1024,512]{1,0:T(8,128)S(1)} %fusion.30, f32[1025,256]{1,0:T(8,128)S(1)} %get-tuple-element.22, f32[1025,256]{1,0:T(8,128)S(1)} %get-tuple-element.21, f32[1025,256]{1,0:T(8,128)S(1)} %get-tuple-element.23, f32[1025,256]{1,0:T(8,128)S(1)} %get-tuple-element.20, f32[2050]{0:T(1024)S(1)} %fusion.35, ...), kind=kOutput, calls=%fused_computation.37 | convolution fusion | flops 2166898688 | bytes 12599304 | tf_op jit(solution)/shard_map/dot_general | solution.py:138
  63.7 2.2 %fusion.17 = f32[1024,256]{1,0:T(8,128)S(1)} fusion(f32[1025,256]{1,0:T(8,128)S(1)} %get-tuple-element.29, f32[1025,256]{1,0:T(8,128)S(1)} %get-tuple-element.28, f32[2050]{0:T(1024)S(1)} %fusion.35, bf16[1025,1024]{1,0:T(8,128)(2,1)S(1)} %copy-done.1, bf16[1025,1024]{1,0:T(8,128)(2,1)S(1)} %copy-done), kind=kOutput, calls=%fused_computation.49 | convolution fusion | flops 1084761600 | bytes 7354376 | tf_op jit(solution)/shard_map/dot_general | solution.py:138
  66.0 2.1 %fusion.16 = f32[1024,256]{1,0:T(8,128)S(1)} fusion(f32[1024,256]{1,0:T(8,128)S(1)} %fusion.17, f32[1025,256]{1,0:T(8,128)S(1)} %get-tuple-element.29, f32[1025,256]{1,0:T(8,128)S(1)} %get-tuple-element.28, f32[2050]{0:T(1024)S(1)} %fusion.35, bf16[1024,256]{1,0:T(8,128)(2,1)S(1)} %get-tuple-element.18, f32[256]{0:T(256)S(1)} %dynamic_slice.7, ...), kind=kOutput, calls=%fused_computation.47 | convolution fusion | flops 1087384576 | bytes 8928264 | tf_op jit(solution)/shard_map/dot_general | solution.py:138
  68.0 0.2 fusion.23
  68.2 1.6 %multiply_bitcast_fusion.1 = (f32[1024,1,256]{2,0,1:T(8,128)S(1)}, f32[1024,1,256]{2,0,1:T(8,128)S(1)}, bf16[1024,256]{1,0:T(8,128)(2,1)}, f32[1024,256]{1,0:T(8,128)}) fusion(f32[1024,3,256]{2,0,1:T(8,128)S(1)} %fusion.7, bf16[1024,256]{1,0:T(8,128)(2,1)S(1)} %get-tuple-element.19, f32[1024,512]{1,0:T(8,128)S(1)} %fusion.15, f32[256]{0:T(256)S(1)} %dynamic_slice.7, ...), kind=kLoop, calls=%fused_computation.70 | loop fusion | flops 1835008 | bytes 10486784 | tf_op jit(solution)/shard_map/stack | solution.py:192
  69.8 1.3 fusion.9
  71.2 0.1 maximum_maximum_fusion
  71.2 1.3 pad_maximum_fusion.6
  72.5 19.2 %all_to_all.15 = f32[8,144,256]{2,1,0:T(8,128)S(1)} all-to-all(f32[8,144,256]{2,1,0:T(8,128)S(1)} %pad_maximum_fusion.6), channel_id=1, replica_groups=mesh['dp'=4,'seq'=8] {'seq'}, dimensions={0} | all-to-all | bytes 2359296 | tf_op jit(solution)/shard_map/all_to_all | solution.py:388
  91.7 0.1 copy.29
  91.8 0.1 slice.135
  91.9 1.2 pad_maximum_fusion.5
  93.1 0.0 reduce-scatter.2.cloned.1.call-update
  93.1 1.0 add_convert_fusion
  94.1 0.0 copy-start.2
  94.1 0.1 copy.38
  94.3 0.9 copy-done.2
  95.2 0.2 pad_maximum_fusion.4
  95.3 29.7 %all_to_all.16.in_ref = bf16[8,4,128,256]{3,2,1,0:T(8,128)(2,1)} all-to-all(bf16[8,4,128,256]{3,2,1,0:T(8,128)(2,1)S(1)} %pad_maximum_fusion.4), channel_id=1, replica_groups=mesh['dp'=4,'seq'=8] {'seq'}, dimensions={0} | all-to-all | bytes 4194304 | tf_op jit(solution)/shard_map/all_to_all | solution.py:366
  125.1 3.6 %shard_map.93 = (bf16[128,2048]{1,0:T(8,128)(2,1)}, bf16[128,6144]{1,0:T(8,128)(2,1)}) custom-call(bf16[8,4,128,256]{3,2,1,0:T(8,128)(2,1)} %all_to_all.16.in_ref), custom_call_target="tpu_custom_call" | custom-call | tf_op jit(solution)/shard_map/pallas_call | solution.py:297
  128.7 0.9 slice.137
  129.6 0.7 reshape.102
  130.4 0.6 copy.36
  131.0 1.0 slice.140
  131.9 0.1 copy.35
  132.1 0.8 copy.34
  (17 shorter events, 0.2 us)
Async XLA Ops:
  11.8 5.4 %copy-start.3 = (f32[3,6144]{1,0:T(4,128)S(1)}, f32[3,6144]{1,0:T(4,128)}, u32[]{:S(2)}) copy-start(f32[3,6144]{1,0:T(4,128)} %param.6) | copy-start | bytes 221188
  11.8 37.6 %all-to-all-start = ((bf16[8,5,128,256]{3,2,1,0:T(8,128)(2,1)}), bf16[8,5,128,256]{3,2,1,0:T(8,128)(2,1)S(1)}, u32[]{:S(2)}, u32[]{:S(2)}) async-start(bf16[8,5,128,256]{3,2,1,0:T(8,128)(2,1)} %shard_map.92), calls=%async_computation | async-start | bytes 5242880 | tf_op jit(solution)/shard_map/all_to_all | solution.py:331
  17.1 111.5 %reduce-scatter.2.cloned.1.call-start = ((), (), s32[]{:S(2)}) async-start(), calls=%async_computation.4 | async-start | bytes 1720320 | tf_op jit(solution)/shard_map/reduce_scatter | solution.py:399
  50.9 1.6 %copy-start = (bf16[1025,1024]{1,0:T(8,128)(2,1)S(1)}, bf16[1025,1024]{1,0:T(8,128)(2,1)}, u32[]{:S(2)}) copy-start(bf16[1025,1024]{1,0:T(8,128)(2,1)} %get-tuple-element.26) | copy-start | bytes 6297604
  50.9 2.2 %copy-start.1 = (bf16[1025,1024]{1,0:T(8,128)(2,1)S(1)}, bf16[1025,1024]{1,0:T(8,128)(2,1)}, u32[]{:S(2)}) copy-start(bf16[1025,1024]{1,0:T(8,128)(2,1)} %get-tuple-element.27) | copy-start | bytes 6297604
  94.1 1.0 copy-start.2
Sparse Core Ops, SparseCore 0:
  93.2 31.6 reduce-scatter.1

commit v7 on v6

--- a/solution.py
+++ b/solution.py
@@ -148,11 +148,8 @@
     row = lax.broadcasted_iota(jnp.int32, (2 * bins, 1), 0)
     edge = (row == 0) | (row == bins - 1) | (row == bins) | (row == 2 * bins - 1)
     weight = jnp.where(edge, 1.0 / fft_length, 2.0 / fft_length)
-    scaled = spectrum * weight
-    spec_high = scaled.astype(jnp.bfloat16)
-    spec_low = (scaled - spec_high.astype(jnp.float32)).astype(jnp.bfloat16)
-    backward = ((0,), (0,))
-    return bf16_dot(table, spec_high, backward) + bf16_dot(table, spec_low, backward)
+    scaled = (spectrum * weight).astype(jnp.bfloat16)
+    return bf16_dot(table, scaled, ((0,), (0,)))
 
 
 def split(spectrum):

time: 140 us -> 135 us (0.964)
  matrix products: 13.8 us -> 8.62 us
    dot_general x6 -> x4, matrix products: 13.8 us -> 8.62 us  [bf16_dot(): lax.dot_general(left, right, (dims, ((), ())), preferred_element_type=jnp...]
  transfers between devices with their start and end apart: 2 -> 2, of which waited for: 1 -> 1; matrix products, arithmetic and copies ran while one was open for 17% -> 18% of each run, Pallas kernels for 3% -> 3%
where the time goes in v7:
time: 135 us; the launch traced here: 134 us
  blocking collectives  48.9 us (36%)
  other arithmetic  30.6 us (23%)
  between operations  14.3 us (11%)
  waiting for transfers between devices  9.64 us (7%)
  matrix products  8.62 us (6%)
  local copies, waits for them, and re-layouts  8.54 us (6%)
  Pallas kernels  8.21 us (6%)
  starting transfers between devices  5.34 us (4%)
    all_to_all x1, blocking collectives, local(): moved_out = lax.all_to_all(joined_out, 'seq', 0, 0, tiled=True)  29.7 us
    all_to_all x1, blocking collectives, local(): moved = lax.all_to_all(chunks, 'seq', 0, 0, tiled=True)  19.2 us
    another operation x1, other arithmetic  17.9 us
    all_to_all x1, waiting for transfers between devices, local(): lax.all_to_all(arranged, 'seq', 0, 0, tiled=True).transpose(0, 2, 1, 3)  9.62 us
    dot_general x4, matrix products, bf16_dot(): lax.dot_general(left, right, (dims, ((), ())), preferred_element_type=jnp...  8.62 us
    all_to_all x1, starting transfers between devices, local(): lax.all_to_all(arranged, 'seq', 0, 0, tiled=True).transpose(0, 2, 1, 3)  5.3 us
    pallas_call x1, Pallas kernels, gather_tiles(): pl.pallas_call(body, grid=(5,), in_specs=[pl.BlockSpec((rows, width), lam...  4.65 us
    unnamed x12, local copies, waits for them, and re-layouts  4.32 us
  transfers between devices with their start and end apart: 2, of which 1 were waited for; matrix products, arithmetic and copies ran while one was open for 18% of the time, Pallas kernels for 3%

profile of v7, /device:TPU:0, one launch (start us, length us, event | category | flops | bytes accessed | tf_op | source)
XLA Modules:
  0.0 134.2 jit_solution(8217580227849688654)
XLA Ops:
  7.2 4.7 %shard_map.92 = bf16[8,5,128,256]{3,2,1,0:T(8,128)(2,1)} custom-call(bf16[128,6144]{1,0:T(8,128)(2,1)} %bitcast.85, bf16[128,2048]{1,0:T(8,128)(2,1)} %bitcast.88, bf16[128,2048]{1,0:T(8,128)(2,1)} %r_ref.1), custom_call_target="tpu_custom_call" | custom-call | tf_op jit(solution)/shard_map/pallas_call | solution.py:264
  11.8 0.0 copy-start.3
  11.8 5.3 %all-to-all-start = ((bf16[8,5,128,256]{3,2,1,0:T(8,128)(2,1)}), bf16[8,5,128,256]{3,2,1,0:T(8,128)(2,1)S(1)}, u32[]{:S(2)}, u32[]{:S(2)}) async-start(bf16[8,5,128,256]{3,2,1,0:T(8,128)(2,1)} %shard_map.92), calls=%async_computation | async-start | bytes 5242880 | tf_op jit(solution)/shard_map/all_to_all | solution.py:328
  17.1 0.0 reduce-scatter.2.cloned.1.call-start
  17.2 0.0 copy-done.3
  17.2 0.1 reshape.90
  17.3 3.7 %add_select_fusion = s32[1025,1024]{1,0:T(8,128)} fusion(), kind=kLoop, calls=%fused_computation | loop fusion | flops 12595200 | bytes 4198400 | tf_op jit(solution)/shard_map/jit(remainder)/select_n | solution.py:130
  21.0 0.8 dynamic_slice.7
  21.7 0.1 pad.8.clone
  21.8 17.9 %cosine_convert_fusion = (bf16[1025,1024]{1,0:T(8,128)(2,1)}, bf16[1025,1024]{1,0:T(8,128)(2,1)}) fusion(s32[1025,1024]{1,0:T(8,128)} %add_select_fusion), kind=kLoop, calls=%fused_computation.5 | loop fusion | flops 5248000 | bytes 8396800 | tf_op jit(solution)/shard_map/convert.1
  39.8 9.6 %all-to-all-done = bf16[8,5,128,256]{3,2,1,0:T(8,128)(2,1)S(1)} async-done(((bf16[8,5,128,256]{3,2,1,0:T(8,128)(2,1)}), bf16[8,5,128,256]{3,2,1,0:T(8,128)(2,1)S(1)}, u32[]{:S(2)}, u32[]{:S(2)}) %all-to-all-start) | async-done | bytes 2621472 | tf_op jit(solution)/shard_map/all_to_all | solution.py:328
  49.4 0.2 copy.27
  49.6 0.1 slice.121
  49.7 1.0 fusion.8
  50.7 0.0 copy-start
  50.8 0.0 copy-start.1
  50.8 0.3 fusion.19
  51.1 1.2 copy-done
  52.3 0.6 copy-done.1
  53.0 1.4 %fusion.33 = f32[2050,256]{1,0:T(8,128)S(1)} fusion(bf16[1024,256]{1,0:T(8,128)(2,1)S(1)} %get-tuple-element.19, bf16[1025,1024]{1,0:T(8,128)(2,1)S(1)} %copy-done.1, bf16[1025,1024]{1,0:T(8,128)(2,1)S(1)} %copy-done), kind=kOutput, calls=%fused_computation.86 | convolution fusion | flops 1083187200 | bytes 6821888 | tf_op jit(solution)/shard_map/dot_general | solution.py:138
  54.4 2.4 %fusion.22 = f32[2050,512]{1,0:T(8,128)S(1)} fusion(bf16[1024,256]{1,0:T(8,128)(2,1)S(1)} %slice_bitcast_fusion.4, bf16[1024,256]{1,0:T(8,128)(2,1)S(1)} %get-tuple-element.18, bf16[1025,1024]{1,0:T(8,128)(2,1)S(1)} %copy-done.1, bf16[1025,1024]{1,0:T(8,128)(2,1)S(1)} %copy-done), kind=kOutput, calls=%fused_computation.59 | convolution fusion | flops 2160074752 | bytes 9445376 | tf_op jit(solution)/shard_map/dot_general | solution.py:138
  56.8 0.3 multiply_subtract_fusion.2
  57.2 0.7 multiply_add_fusion.1
  57.8 2.0 %convolution_add_fusion = f32[1024,256]{1,0:T(8,128)S(1)} fusion(f32[1025,256]{1,0:T(8,128)S(1)} %get-tuple-element.29, f32[1025,256]{1,0:T(8,128)S(1)} %get-tuple-element.28, f32[2050]{0:T(1024)S(1)} %fusion.29, bf16[1024,256]{1,0:T(8,128)(2,1)S(1)} %get-tuple-element.18, f32[256]{0:T(256)S(1)} %dynamic_slice.7, bf16[1025,1024]{1,0:T(8,128)(2,1)S(1)} %copy-done.1, ...), kind=kOutput, calls=%fused_computation.43 | convolution fusion | flops 1085548032 | bytes 7879688 | tf_op jit(solution)/shard_map/dot_general | solution.py:138
  59.8 0.1 fusion.20
  59.9 2.8 %fusion.12 = f32[1024,512]{1,0:T(8,128)S(1)} fusion(f32[1025,256]{1,0:T(8,128)S(1)} %get-tuple-element.22, f32[1025,256]{1,0:T(8,128)S(1)} %get-tuple-element.21, f32[1025,256]{1,0:T(8,128)S(1)} %get-tuple-element.23, f32[1025,256]{1,0:T(8,128)S(1)} %get-tuple-element.20, f32[2050]{0:T(1024)S(1)} %fusion.29, bf16[1025,1024]{1,0:T(8,128)(2,1)S(1)} %copy-done.1, ...), kind=kOutput, calls=%fused_computation.29 | convolution fusion | flops 2163225600 | bytes 10502152 | tf_op jit(solution)/shard_map/dot_general | solution.py:138
  62.7 1.5 %multiply_bitcast_fusion.1 = (f32[1024,1,256]{2,0,1:T(8,128)S(1)}, f32[1024,1,256]{2,0,1:T(8,128)S(1)}, bf16[1024,256]{1,0:T(8,128)(2,1)}, f32[1024,256]{1,0:T(8,128)}) fusion(f32[1024,3,256]{2,0,1:T(8,128)S(1)} %fusion.8, bf16[1024,256]{1,0:T(8,128)(2,1)S(1)} %get-tuple-element.19, f32[1024,512]{1,0:T(8,128)S(1)} %fusion.12, f32[256]{0:T(256)S(1)} %dynamic_slice.7, ...), kind=kLoop, calls=%fused_computation.64 | loop fusion | flops 1835008 | bytes 10486784 | tf_op jit(solution)/shard_map/stack | solution.py:189
  64.3 1.3 fusion.10
  65.6 0.1 maximum_maximum_fusion
  65.7 1.3 pad_maximum_fusion.6
  67.0 19.2 %all_to_all.15 = f32[8,144,256]{2,1,0:T(8,128)S(1)} all-to-all(f32[8,144,256]{2,1,0:T(8,128)S(1)} %pad_maximum_fusion.6), channel_id=1, replica_groups=mesh['dp'=4,'seq'=8] {'seq'}, dimensions={0} | all-to-all | bytes 2359296 | tf_op jit(solution)/shard_map/all_to_all | solution.py:385
  86.2 0.1 copy.29
  86.2 0.1 slice.135
  86.4 1.2 pad_maximum_fusion.5
  87.5 0.0 reduce-scatter.2.cloned.1.call-update
  87.6 1.0 add_convert_fusion
  88.5 0.0 copy-start.2
  88.5 0.1 copy.38
  88.7 0.9 copy-done.2
  89.6 0.2 pad_maximum_fusion.4
  89.8 29.7 %all_to_all.16.in_ref = bf16[8,4,128,256]{3,2,1,0:T(8,128)(2,1)} all-to-all(bf16[8,4,128,256]{3,2,1,0:T(8,128)(2,1)S(1)} %pad_maximum_fusion.4), channel_id=1, replica_groups=mesh['dp'=4,'seq'=8] {'seq'}, dimensions={0} | all-to-all | bytes 4194304 | tf_op jit(solution)/shard_map/all_to_all | solution.py:363
  119.5 3.6 %shard_map.93 = (bf16[128,2048]{1,0:T(8,128)(2,1)}, bf16[128,6144]{1,0:T(8,128)(2,1)}) custom-call(bf16[8,4,128,256]{3,2,1,0:T(8,128)(2,1)} %all_to_all.16.in_ref), custom_call_target="tpu_custom_call" | custom-call | tf_op jit(solution)/shard_map/pallas_call | solution.py:294
  123.1 0.9 slice.137
  124.1 0.7 reshape.102
  124.8 0.6 copy.36
  125.4 1.0 slice.140
  126.4 0.1 copy.35
  126.5 0.8 copy.34
  (15 shorter events, 0.2 us)
Async XLA Ops:
  11.8 5.4 %copy-start.3 = (f32[3,6144]{1,0:T(4,128)S(1)}, f32[3,6144]{1,0:T(4,128)}, u32[]{:S(2)}) copy-start(f32[3,6144]{1,0:T(4,128)} %param.6) | copy-start | bytes 221188
  11.8 37.6 %all-to-all-start = ((bf16[8,5,128,256]{3,2,1,0:T(8,128)(2,1)}), bf16[8,5,128,256]{3,2,1,0:T(8,128)(2,1)S(1)}, u32[]{:S(2)}, u32[]{:S(2)}) async-start(bf16[8,5,128,256]{3,2,1,0:T(8,128)(2,1)} %shard_map.92), calls=%async_computation | async-start | bytes 5242880 | tf_op jit(solution)/shard_map/all_to_all | solution.py:328
  17.1 106.0 %reduce-scatter.2.cloned.1.call-start = ((), (), s32[]{:S(2)}) async-start(), calls=%async_computation.4 | async-start | bytes 1720320 | tf_op jit(solution)/shard_map/reduce_scatter | solution.py:396
  50.7 1.6 %copy-start = (bf16[1025,1024]{1,0:T(8,128)(2,1)S(1)}, bf16[1025,1024]{1,0:T(8,128)(2,1)}, u32[]{:S(2)}) copy-start(bf16[1025,1024]{1,0:T(8,128)(2,1)} %get-tuple-element.26) | copy-start | bytes 6297604
  50.8 2.2 %copy-start.1 = (bf16[1025,1024]{1,0:T(8,128)(2,1)S(1)}, bf16[1025,1024]{1,0:T(8,128)(2,1)}, u32[]{:S(2)}) copy-start(bf16[1025,1024]{1,0:T(8,128)(2,1)} %get-tuple-element.27) | copy-start | bytes 6297604
  88.5 1.0 copy-start.2
Sparse Core Ops, SparseCore 0:
  87.7 31.6 reduce-scatter.1

commit v8 on v7

--- a/solution.py
+++ b/solution.py
@@ -171,9 +171,8 @@
     key_feat = mixed[:, 1]
     value_feat = mixed[:, 2]
     product = (key_feat * value_feat).astype(jnp.bfloat16)
-    first = to_spectrum(tables, jnp.concatenate([product, resp], axis=1))
-    prod_re, prod_im = split(first[:, :narrow])
-    resp_re, resp_im = split(first[:, narrow:])
+    prod_re, prod_im = split(to_spectrum(tables, product))
+    resp_re, resp_im = split(to_spectrum(tables, resp))
     conv_out = to_signal(
         tables, join(prod_re * resp_re - prod_im * resp_im, prod_re * resp_im + prod_im * resp_re)
     )

time: 135 us -> 135 us (level)
    dot_general x4 -> x5, matrix products: 8.62 us -> 9 us  [bf16_dot(): lax.dot_general(left, right, (dims, ((), ())), preferred_element_type=jnp...]
where the time goes in v8:
time: 135 us
  blocking collectives  48.9 us (36%)
  other arithmetic  30.5 us (23%)
  between operations  14.3 us (11%)
  waiting for transfers between devices  9.82 us (7%)
  matrix products  9 us (7%)
  local copies, waits for them, and re-layouts  8.51 us (6%)
  Pallas kernels  8.21 us (6%)
  starting transfers between devices  5.34 us (4%)
    all_to_all x1, blocking collectives, local(): moved_out = lax.all_to_all(joined_out, 'seq', 0, 0, tiled=True)  29.7 us
    all_to_all x1, blocking collectives, local(): moved = lax.all_to_all(chunks, 'seq', 0, 0, tiled=True)  19.2 us
    another operation x1, other arithmetic  17.8 us
    all_to_all x1, waiting for transfers between devices, local(): lax.all_to_all(arranged, 'seq', 0, 0, tiled=True).transpose(0, 2, 1, 3)  9.81 us
    dot_general x5, matrix products, bf16_dot(): lax.dot_general(left, right, (dims, ((), ())), preferred_element_type=jnp...  9 us
    all_to_all x1, starting transfers between devices, local(): lax.all_to_all(arranged, 'seq', 0, 0, tiled=True).transpose(0, 2, 1, 3)  5.3 us
    pallas_call x1, Pallas kernels, gather_tiles(): pl.pallas_call(body, grid=(5,), in_specs=[pl.BlockSpec((rows, width), lam...  4.65 us
    unnamed x12, local copies, waits for them, and re-layouts  4.32 us
  transfers between devices with their start and end apart: 2, of which 1 were waited for; matrix products, arithmetic and copies ran while one was open for 18% of the time, Pallas kernels for 3%

profile of v8, /device:TPU:0, one launch (start us, length us, event | category | flops | bytes accessed | tf_op | source)
XLA Modules:
  0.0 134.6 jit_solution(10880689426501495804)
XLA Ops:
  7.2 4.7 %shard_map.92 = bf16[8,5,128,256]{3,2,1,0:T(8,128)(2,1)} custom-call(bf16[128,6144]{1,0:T(8,128)(2,1)} %bitcast.87, bf16[128,2048]{1,0:T(8,128)(2,1)} %bitcast.90, bf16[128,2048]{1,0:T(8,128)(2,1)} %r_ref.1), custom_call_target="tpu_custom_call" | custom-call | tf_op jit(solution)/shard_map/pallas_call | solution.py:263
  11.8 5.3 %all-to-all-start = ((bf16[8,5,128,256]{3,2,1,0:T(8,128)(2,1)}), bf16[8,5,128,256]{3,2,1,0:T(8,128)(2,1)S(1)}, u32[]{:S(2)}, u32[]{:S(2)}) async-start(bf16[8,5,128,256]{3,2,1,0:T(8,128)(2,1)} %shard_map.92), calls=%async_computation | async-start | bytes 5242880 | tf_op jit(solution)/shard_map/all_to_all | solution.py:327
  17.1 0.0 reduce-scatter.2.cloned.1.call-start
  17.2 0.0 copy-done.3
  17.2 0.1 reshape.90
  17.3 3.7 %add_select_fusion = s32[1025,1024]{1,0:T(8,128)} fusion(), kind=kLoop, calls=%fused_computation | loop fusion | flops 12595200 | bytes 4198400 | tf_op jit(solution)/shard_map/jit(remainder)/select_n | solution.py:130
  21.0 0.8 dynamic_slice.7
  21.7 0.1 pad.8.clone
  21.8 17.8 %cosine_convert_fusion = (bf16[1025,1024]{1,0:T(8,128)(2,1)}, bf16[1025,1024]{1,0:T(8,128)(2,1)}) fusion(s32[1025,1024]{1,0:T(8,128)} %add_select_fusion), kind=kLoop, calls=%fused_computation.5 | loop fusion | flops 5248000 | bytes 8396800 | tf_op jit(solution)/shard_map/convert.1
  39.6 9.8 %all-to-all-done = bf16[8,5,128,256]{3,2,1,0:T(8,128)(2,1)S(1)} async-done(((bf16[8,5,128,256]{3,2,1,0:T(8,128)(2,1)}), bf16[8,5,128,256]{3,2,1,0:T(8,128)(2,1)S(1)}, u32[]{:S(2)}, u32[]{:S(2)}) %all-to-all-start) | async-done | bytes 2621472 | tf_op jit(solution)/shard_map/all_to_all | solution.py:327
  49.4 0.2 copy.27
  49.6 0.1 slice.115
  49.7 1.0 fusion.8
  50.7 0.0 copy-start
  50.7 0.0 copy-start.1
  50.7 0.3 fusion.19
  51.1 1.2 copy-done
  52.3 0.6 copy-done.1
  52.9 1.4 %fusion.22 = f32[2050,256]{1,0:T(8,128)S(1)} fusion(bf16[1024,5,256]{2,0,1:T(8,128)(2,1)S(1)} %bitcast.79, bf16[1025,1024]{1,0:T(8,128)(2,1)S(1)} %copy-done.1, bf16[1025,1024]{1,0:T(8,128)(2,1)S(1)} %copy-done), kind=kOutput, calls=%fused_computation.65 | convolution fusion | flops 1083187200 | bytes 6850560 | tf_op jit(solution)/shard_map/dot_general | solution.py:138
  54.3 1.4 %fusion.29 = f32[2050,256]{1,0:T(8,128)S(1)} fusion(bf16[1024,256]{1,0:T(8,128)(2,1)S(1)} %get-tuple-element.19, bf16[1025,1024]{1,0:T(8,128)(2,1)S(1)} %copy-done.1, bf16[1025,1024]{1,0:T(8,128)(2,1)S(1)} %copy-done), kind=kOutput, calls=%fused_computation.82 | convolution fusion | flops 1083187200 | bytes 6821888 | tf_op jit(solution)/shard_map/dot_general | solution.py:138
  55.8 1.4 %fusion.30 = f32[2050,256]{1,0:T(8,128)S(1)} fusion(bf16[1024,256]{1,0:T(8,128)(2,1)S(1)} %get-tuple-element.18, bf16[1025,1024]{1,0:T(8,128)(2,1)S(1)} %copy-done.1, bf16[1025,1024]{1,0:T(8,128)(2,1)S(1)} %copy-done), kind=kOutput, calls=%fused_computation.83 | convolution fusion | flops 1083187200 | bytes 6821888 | tf_op jit(solution)/shard_map/dot_general | solution.py:138
  57.2 0.3 multiply_add_fusion.1
  57.5 0.7 multiply_subtract_fusion.2
  58.3 2.0 %convolution_add_fusion = f32[1024,256]{1,0:T(8,128)S(1)} fusion(f32[1025,256]{1,0:T(8,128)S(1)} %get-tuple-element.25, f32[1025,256]{1,0:T(8,128)S(1)} %get-tuple-element.24, f32[2050]{0:T(1024)S(1)} %fusion.26, bf16[1024,256]{1,0:T(8,128)(2,1)S(1)} %get-tuple-element.18, f32[256]{0:T(256)S(1)} %dynamic_slice.7, bf16[1025,1024]{1,0:T(8,128)(2,1)S(1)} %copy-done.1, ...), kind=kOutput, calls=%fused_computation.43 | convolution fusion | flops 1085548032 | bytes 7879688 | tf_op jit(solution)/shard_map/dot_general | solution.py:138
  60.3 0.1 fusion.20
  60.4 2.8 %fusion.12 = f32[1024,512]{1,0:T(8,128)S(1)} fusion(f32[1025,256]{1,0:T(8,128)S(1)} %get-tuple-element.32, f32[1025,256]{1,0:T(8,128)S(1)} %get-tuple-element.33, f32[1025,256]{1,0:T(8,128)S(1)} %get-tuple-element.27, f32[1025,256]{1,0:T(8,128)S(1)} %get-tuple-element.26, f32[2050]{0:T(1024)S(1)} %fusion.26, bf16[1025,1024]{1,0:T(8,128)(2,1)S(1)} %copy-done.1, ...), kind=kOutput, calls=%fused_computation.29 | convolution fusion | flops 2163225600 | bytes 10502152 | tf_op jit(solution)/shard_map/dot_general | solution.py:138
  63.2 1.5 %multiply_bitcast_fusion.1 = (f32[1024,1,256]{2,0,1:T(8,128)S(1)}, f32[1024,1,256]{2,0,1:T(8,128)S(1)}, bf16[1024,256]{1,0:T(8,128)(2,1)}, f32[1024,256]{1,0:T(8,128)}) fusion(f32[1024,3,256]{2,0,1:T(8,128)S(1)} %fusion.8, bf16[1024,256]{1,0:T(8,128)(2,1)S(1)} %get-tuple-element.19, f32[1024,512]{1,0:T(8,128)S(1)} %fusion.12, f32[256]{0:T(256)S(1)} %dynamic_slice.7, ...), kind=kLoop, calls=%fused_computation.60 | loop fusion | flops 1835008 | bytes 10486784 | tf_op jit(solution)/shard_map/stack | solution.py:188
  64.7 1.3 fusion.10
  66.0 0.1 maximum_maximum_fusion
  66.1 1.3 pad_maximum_fusion.6
  67.4 19.2 %all_to_all.15 = f32[8,144,256]{2,1,0:T(8,128)S(1)} all-to-all(f32[8,144,256]{2,1,0:T(8,128)S(1)} %pad_maximum_fusion.6), channel_id=1, replica_groups=mesh['dp'=4,'seq'=8] {'seq'}, dimensions={0} | all-to-all | bytes 2359296 | tf_op jit(solution)/shard_map/all_to_all | solution.py:384
  86.6 0.1 copy.29
  86.7 0.1 slice.129
  86.8 1.2 pad_maximum_fusion.5
  88.0 0.0 reduce-scatter.2.cloned.1.call-update
  88.0 1.0 add_convert_fusion
  89.0 0.0 copy-start.2
  89.0 0.1 copy.38
  89.1 0.9 copy-done.2
  90.0 0.2 pad_maximum_fusion.4
  90.2 29.7 %all_to_all.16.in_ref = bf16[8,4,128,256]{3,2,1,0:T(8,128)(2,1)} all-to-all(bf16[8,4,128,256]{3,2,1,0:T(8,128)(2,1)S(1)} %pad_maximum_fusion.4), channel_id=1, replica_groups=mesh['dp'=4,'seq'=8] {'seq'}, dimensions={0} | all-to-all | bytes 4194304 | tf_op jit(solution)/shard_map/all_to_all | solution.py:362
  119.9 3.6 %shard_map.93 = (bf16[128,2048]{1,0:T(8,128)(2,1)}, bf16[128,6144]{1,0:T(8,128)(2,1)}) custom-call(bf16[8,4,128,256]{3,2,1,0:T(8,128)(2,1)} %all_to_all.16.in_ref), custom_call_target="tpu_custom_call" | custom-call | tf_op jit(solution)/shard_map/pallas_call | solution.py:293
  123.5 0.9 slice.131
  124.5 1.0 slice.134
  125.5 0.1 copy.35
  125.6 0.8 copy.34
  126.4 0.7 reshape.102
  127.2 0.6 copy.36
  (15 shorter events, 0.2 us)
Async XLA Ops:
  11.8 5.4 %copy-start.3 = (f32[3,6144]{1,0:T(4,128)S(1)}, f32[3,6144]{1,0:T(4,128)}, u32[]{:S(2)}) copy-start(f32[3,6144]{1,0:T(4,128)} %param.6) | copy-start | bytes 221188
  11.8 37.6 %all-to-all-start = ((bf16[8,5,128,256]{3,2,1,0:T(8,128)(2,1)}), bf16[8,5,128,256]{3,2,1,0:T(8,128)(2,1)S(1)}, u32[]{:S(2)}, u32[]{:S(2)}) async-start(bf16[8,5,128,256]{3,2,1,0:T(8,128)(2,1)} %shard_map.92), calls=%async_computation | async-start | bytes 5242880 | tf_op jit(solution)/shard_map/all_to_all | solution.py:327
  17.1 106.4 %reduce-scatter.2.cloned.1.call-start = ((), (), s32[]{:S(2)}) async-start(), calls=%async_computation.4 | async-start | bytes 1720320 | tf_op jit(solution)/shard_map/reduce_scatter | solution.py:395
  50.7 1.6 %copy-start = (bf16[1025,1024]{1,0:T(8,128)(2,1)S(1)}, bf16[1025,1024]{1,0:T(8,128)(2,1)}, u32[]{:S(2)}) copy-start(bf16[1025,1024]{1,0:T(8,128)(2,1)} %get-tuple-element.22) | copy-start | bytes 6297604
  50.7 2.2 %copy-start.1 = (bf16[1025,1024]{1,0:T(8,128)(2,1)S(1)}, bf16[1025,1024]{1,0:T(8,128)(2,1)}, u32[]{:S(2)}) copy-start(bf16[1025,1024]{1,0:T(8,128)(2,1)} %get-tuple-element.23) | copy-start | bytes 6297604
  89.0 1.0 copy-start.2
Sparse Core Ops, SparseCore 0:
  88.1 31.6 reduce-scatter.1
